TPU v7x, 512 devices: a whole 4x8x8 slice. The times are simulated.
512 devices in a mesh: space: 32 (over y, x_lo, core), modes: 16 (over z, x_hi).
Axes of the slice: x: 4 (x_hi: 2, x_lo: 2; x = x_hi * 2 + x_lo), y: 8, z: 8, core: 2. Of those that a mesh axis runs over, the one named last changes fastest.
Arguments:
- rhs: bfloat16 [2, 256, 512, 512], P(None, 'modes', 'space'), may hold values from -6 to 6
- initial: bfloat16 [2, 256, 512, 512], P(None, 'modes', 'space'), may hold values from -6 to 6
- region: int32 [512, 512], P('space'), may hold values from 0 to 7
- base_table: float32 [2, 8], replicated, may hold values from 0.5 to 4
- term_table: float32 [2, 3, 8], replicated, may hold values from -0.3 to 0.3
- galerkin: bfloat16 [3, 256, 256], replicated, may hold values from -0.375 to 0.375
- block_mask: int32 [3, 16, 16], replicated, may hold values from 0 to 1, as said below
- block_inverse: float32 [16, 16, 16], P('modes'), as said below
Outputs:
- solution: float32 [2, 256, 512, 512], P(None, 'modes', 'space')
Inputs may be any that keep to these rules, and one draw needn't show every extreme that they name: `block_mask`: each mode block is coupled with itself by every term, and some pairs of mode blocks are not coupled. `block_inverse`: blocks near the identity, off-diagonal entries at most 0.3 in magnitude.
All inputs are finite; a program needn't handle non-finite values.
Results may differ from a plain program's by a relative error of at most 0.0017.
Values may be sent and summed in bfloat16 or wider, within the bound.
No kernel may reach another device: no remote copies, remote signals or barrier semaphores. Data moves between devices by JAX's collectives and lax.ppermute only.
A program may use at most 64 MiB of HBM per device.

v0:
```python
import jax
import jax.numpy as jnp
from jax import lax
from jax.sharding import PartitionSpec as P

SWEEPS = 2
LANES = 128


def ring_halo(block, axis, dim):
    count = lax.axis_size(axis)
    forward = [(i, (i + 1) % count) for i in range(count)]
    backward = [(target, source) for source, target in forward]
    low = lax.ppermute(lax.slice_in_dim(block, block.shape[dim] - 1, None, axis=dim), axis, forward)
    high = lax.ppermute(lax.slice_in_dim(block, 0, 1, axis=dim), axis, backward)
    return jnp.concatenate([low, block, high], axis=dim)


def lookup(table, region):
    total = jnp.zeros(table.shape[:-1] + region.shape, jnp.float32)
    for which in range(table.shape[-1]):
        total = total + table[..., which, None, None] * (region == which).astype(jnp.float32)
    return total


def laplace_rows(padded, fill_left, fill_right):
    center = padded[:, 1:-1]
    right = jnp.concatenate([center[..., 1:], fill_right[..., None]], -1)
    left = jnp.concatenate([fill_left[..., None], center[..., :-1]], -1)
    return 4.0 * center - padded[:, 2:] - padded[:, :-2] - right - left


def sweeps(rhs, initial, region, base_table, term_table, galerkin, block_mask, block_inverse):
    terms = galerkin.shape[0]
    modes_all = galerkin.shape[1]
    blocks = block_mask.shape[1]
    width = modes_all // blocks
    shaped = galerkin.reshape(terms, blocks, width, blocks, width)
    coupling = (shaped * block_mask[:, :, None, :, None].astype(jnp.bfloat16)).reshape(
        terms, modes_all, modes_all
    )
    coupling = coupling.transpose(1, 0, 2).reshape(modes_all, terms * modes_all)

    fields, modes_dev = rhs.shape[:2]
    rows, cols = region.shape
    devs = lax.axis_size("modes")
    spaces = lax.axis_size("space")
    col_chunks = cols // LANES
    row_chunks = devs // col_chunks
    rows_c = rows // row_chunks
    me = lax.axis_index("modes")
    my_r = me // col_chunks
    my_c = me % col_chunks

    inv_hi = lax.optimization_barrier(block_inverse[0].astype(jnp.bfloat16))
    rest = block_inverse[0] - inv_hi.astype(jnp.float32)
    inv_mid = lax.optimization_barrier(rest.astype(jnp.bfloat16))
    inv_lo = (rest - inv_mid.astype(jnp.float32)).astype(jnp.bfloat16)
    inv_code = jnp.concatenate([inv_hi, inv_mid, inv_lo], axis=-1)

    base = lax.dynamic_slice(
        lookup(base_table, region), (0, my_r * rows_c, my_c * LANES), (fields, rows_c, LANES)
    )[:, :, None, :]
    coef = lax.dynamic_slice(
        lookup(term_table, region),
        (0, 0, my_r * rows_c, my_c * LANES),
        (fields, terms, rows_c, LANES),
    )
    coef = coef.transpose(0, 2, 1, 3)[:, :, :, None, :]
    inverse_base = 1.0 / (4.0 * base)

    rp = rhs.reshape(fields, modes_dev, row_chunks, rows_c, col_chunks, LANES)
    rp = rp.transpose(2, 4, 0, 3, 1, 5).reshape(devs, fields, rows_c, modes_dev, LANES)
    rhs_c = lax.all_to_all(rp, "modes", split_axis=0, concat_axis=3, tiled=True)[0]
    rhs_c = rhs_c.astype(jnp.float32)

    init_x = ring_halo(initial.transpose(0, 2, 1, 3), "space", 1)

    flat = ("space", "modes")
    total_rc = spaces * row_chunks

    def dev_of(g, c):
        s, r = divmod(g % total_rc, row_chunks)
        return s * devs + r * col_chunks + c

    down = [(dev_of(g, c), dev_of(g + 1, c)) for g in range(total_rc) for c in range(col_chunks)]
    up = [(b, a) for a, b in down]
    rightward = [
        (s * devs + r * col_chunks + c, s * devs + r * col_chunks + c + 1)
        for s in range(spaces)
        for r in range(row_chunks)
        for c in range(col_chunks - 1)
    ]
    leftward = [(b, a) for a, b in rightward]

    def pack(init_f):
        top = init_f[:, 0 : rows : rows_c]
        mid = init_f[:, 1 : rows + 1].reshape(fields, row_chunks, rows_c, modes_dev, cols)
        bot = init_f[:, rows_c + 1 : rows + 2 : rows_c]
        main = jnp.concatenate([top[:, :, None], mid, bot[:, :, None]], axis=2)
        main = main.reshape(fields, row_chunks, rows_c + 2, modes_dev, col_chunks, LANES)
        inner = init_f[:, 1 : rows + 1]
        hl = jnp.pad(inner[..., LANES - 1 : cols - 1 : LANES], ((0, 0), (0, 0), (0, 0), (1, 0)))
        hr = jnp.pad(inner[..., LANES : cols : LANES], ((0, 0), (0, 0), (0, 0), (0, 1)))
        sides = []
        for h in (hl, hr):
            h = h.reshape(fields, row_chunks, rows_c, modes_dev, col_chunks)
            sides.append(h.transpose(0, 1, 3, 4, 2))
        code = jnp.broadcast_to(
            inv_code[None, None, :, None, :], sides[0].shape[:-1] + inv_code.shape[-1:]
        )
        side = jnp.concatenate(sides + [code], axis=-1)
        side = jnp.pad(side, ((0, 0),) * 4 + ((0, LANES - side.shape[-1]),))[:, :, None]
        full = jnp.concatenate([main, side], axis=2)
        full = full.transpose(1, 4, 0, 2, 3, 5).reshape(devs, fields, -1, modes_dev, LANES)
        return lax.all_to_all(full, "modes", split_axis=0, concat_axis=3, tiled=True)[0]

    got = pack(init_x)
    padded = got[:, : rows_c + 2].astype(jnp.float32)
    side = got[:, rows_c + 2].astype(jnp.float32)
    fill_l = side[..., :rows_c].transpose(0, 2, 1)
    fill_r = side[..., rows_c : 2 * rows_c].transpose(0, 2, 1)
    code = side[0, :, 2 * rows_c : 2 * rows_c + 3 * width]
    every = (code[:, :width] + code[:, width : 2 * width]) + code[:, 2 * width :]
    every = every.reshape(blocks, width, width)
    eye = jnp.eye(blocks, dtype=jnp.float32)
    dense_inv = (every[:, :, None, :] * eye[:, None, :, None]).reshape(modes_all, modes_all)
    u_field = padded[:, 1:-1]

    def to_owner(mixed):
        mixed = mixed.reshape(fields, rows_c, devs, modes_dev, LANES)
        back = lax.all_to_all(mixed, "modes", split_axis=2, concat_axis=2, tiled=True)
        back = back.reshape(fields, rows_c, row_chunks, col_chunks, modes_dev, LANES)
        return back.transpose(0, 2, 1, 4, 3, 5).reshape(fields, rows, modes_dev, cols)

    coupled_owner = []
    for sweep in range(SWEEPS):
        if sweep > 0:
            low = lax.ppermute(u_field[:, -1:], flat, down)
            high = lax.ppermute(u_field[:, :1], flat, up)
            fill_l = lax.ppermute(u_field[..., -1], flat, rightward)
            fill_r = lax.ppermute(u_field[..., 0], flat, leftward)
            padded = jnp.concatenate([low, u_field, high], axis=1)
            rounded = lax.optimization_barrier(
                (padded.astype(jnp.bfloat16), fill_l.astype(jnp.bfloat16), fill_r.astype(jnp.bfloat16))
            )
            lap_r = laplace_rows(*(part.astype(jnp.float32) for part in rounded))
        else:
            lap = laplace_rows(padded, fill_l, fill_r)
            lap_r = lap
        tiles = (coef * lap_r[:, :, None]).astype(jnp.bfloat16)
        tiles = tiles.reshape(fields, rows_c, terms * modes_all, LANES)
        coupled = jnp.einsum(
            "ic,fxcy->fxiy", coupling, tiles, preferred_element_type=jnp.float32
        ).astype(jnp.bfloat16)
        coupled_owner.append(to_owner(coupled))
        if sweep < SWEEPS - 1:
            resid = rhs_c - base * lap - coupled.astype(jnp.float32)
            scaled = resid * inverse_base
            update = jnp.einsum(
                "ij,fxjy->fxiy", dense_inv, scaled, precision=lax.Precision.HIGHEST
            )
            u_field = u_field + 0.6 * update

    base_o = lookup(base_table, region)[:, :, None, :]
    inv_base_o = 1.0 / (4.0 * base_o)
    rhs_o = rhs.transpose(0, 2, 1, 3).astype(jnp.float32)
    own_inv = block_inverse[0]
    pad_o = init_x.astype(jnp.float32)
    u_o = pad_o[:, 1:-1]
    zeros = jnp.zeros(u_o.shape[:-1], jnp.float32)
    for sweep in range(SWEEPS):
        if sweep > 0:
            pad_o = ring_halo(u_o, "space", 1)
        lap_o = laplace_rows(pad_o, zeros, zeros)
        resid = rhs_o - base_o * lap_o - coupled_owner[sweep].astype(jnp.float32)
        scaled = resid * inv_base_o
        update = jnp.einsum("ac,fxcy->fxay", own_inv, scaled, precision=lax.Precision.HIGHEST)
        u_o = u_o + 0.6 * update
    return u_o.transpose(0, 2, 1, 3)


def solution(mesh):
    in_specs = (
        P(None, "modes", "space", None),
        P(None, "modes", "space", None),
        P("space", None),
        P(),
        P(),
        P(),
        P(),
        P("modes", None, None),
    )
    out_specs = P(None, "modes", "space", None)
    return jax.shard_map(sweeps, mesh=mesh, in_specs=in_specs, out_specs=out_specs, check_vma=False)
```

profile of v0, /device:TPU:24, one launch (start us, length us, event | category | flops | bytes accessed | tf_op | source)
XLA Modules:
  0.0 156.6 jit_solution(15676658966840952428)
XLA Ops:
  0.0 1.3 copy.159
  1.3 1.9 %collective-permute-start = (bf16[2,1,16,512]{3,2,1,0:T(8,128)(2,1)S(1)}, bf16[2,1,16,512]{3,2,1,0:T(8,128)(2,1)S(1)}, u32[]{:S(2)}, u32[]{:S(2)}) collective-permute-start(bf16[2,1,16,512]{3,2,1,0:T(8,128)(2,1)S(1)} %get-tuple-element.41), channel_id=1, source_target_pairs={{0,16},{16,32},{32,48},{48,64},{64,80},{80,96},{96,112},{112,128},... | collective-permute-start | bytes 98312 | tf_op jit(solution)/shard_map/ppermute | solution.py:14
  3.3 4.5 %collective-permute-start.1 = (bf16[2,1,16,512]{3,2,1,0:T(8,128)(2,1)S(1)}, bf16[2,1,16,512]{3,2,1,0:T(8,128)(2,1)S(1)}, u32[]{:S(2)}, u32[]{:S(2)}) collective-permute-start(bf16[2,1,16,512]{3,2,1,0:T(8,128)(2,1)S(1)} %get-tuple-element.42), channel_id=1, source_target_pairs={{16,0},{32,16},{48,32},{64,48},{80,64},{96,80},{112,96},{128,112},... | collective-permute-start | bytes 98312 | tf_op jit(solution)/shard_map/ppermute | solution.py:15
  7.8 1.2 reshape.133
  9.0 1.2 copy.124
  10.2 12.9 %all-to-all-start.2 = ((bf16[16,2,4,16,128]{4,3,2,1,0:T(8,128)(2,1)}), bf16[16,2,4,16,128]{4,3,2,1,0:T(8,128)(2,1)S(1)}, u32[]{:S(2)}, u32[]{:S(2)}) async-start(bf16[16,2,4,16,128]{4,3,2,1,0:T(8,128)(2,1)} %bitcast.44), calls=%async_computation.2 | async-start | bytes 1048576 | tf_op jit(solution)/shard_map/all_to_all | solution.py:74
  24.3 0.9 copy.112
  25.2 0.9 copy.113
  27.0 0.7 maximum_bitcast_fusion
  27.7 1.1 copy.116
  28.8 11.9 %all-to-all-done.2 = bf16[16,2,4,16,128]{4,3,2,1,0:T(8,128)(2,1)S(1)} async-done(((bf16[16,2,4,16,128]{4,3,2,1,0:T(8,128)(2,1)}), bf16[16,2,4,16,128]{4,3,2,1,0:T(8,128)(2,1)S(1)}, u32[]{:S(2)}, u32[]{:S(2)}) %all-to-all-start.2) | async-done | bytes 524320 | tf_op jit(solution)/shard_map/all_to_all | solution.py:74
  40.7 3.6 %all-to-all-start = ((bf16[16,2,7,16,128]{4,3,2,1,0:T(8,128)(2,1)}), bf16[16,2,7,16,128]{4,3,2,1,0:T(8,128)(2,1)S(1)}, u32[]{:S(2)}, u32[]{:S(2)}) async-start(bf16[16,2,7,16,128]{4,3,2,1,0:T(8,128)(2,1)} %bitcast.20), calls=%async_computation | async-start | bytes 1835008 | tf_op jit(solution)/shard_map/all_to_all | solution.py:116
  45.7 2.1 %mul.582 = bf16[3,16,16,16,16]{4,3,2,1,0:T(8,128)(2,1)} broadcast(bf16[3,16,16]{2,1,0:T(8,128)(2,1)S(1)} %convert_element_type.179), dimensions={0,1,3} | broadcast | bytes 394752 | tf_op jit(solution)/shard_map/mul | solution.py:39
  47.8 5.1 %mul.583 = bf16[3,256,256]{2,1,0:T(8,128)(2,1)} reshape(bf16[3,16,16,16,16]{4,3,2,1,0:T(8,128)(2,1)} %mul.582) | data formatting | bytes 786432 | tf_op jit(solution)/shard_map/mul | solution.py:39
  53.2 0.8 multiply_divide_fusion
  56.1 1.1 bitcast_convert_fusion
  57.2 1.3 copy.126
  58.6 10.6 %all-to-all-done = bf16[16,2,7,16,128]{4,3,2,1,0:T(8,128)(2,1)S(1)} async-done(((bf16[16,2,7,16,128]{4,3,2,1,0:T(8,128)(2,1)}), bf16[16,2,7,16,128]{4,3,2,1,0:T(8,128)(2,1)S(1)}, u32[]{:S(2)}, u32[]{:S(2)}) %all-to-all-start) | async-done | bytes 917536 | tf_op jit(solution)/shard_map/all_to_all | solution.py:116
  69.4 0.9 copy-done.2
  70.7 1.5 fusion.99
  72.3 0.9 slice.250
  73.6 1.6 %broadcast_multiply_fusion = f32[16,16,16,16]{3,2,1,0:T(8,128)} fusion(f32[16,16]{1,0:T(8,128)S(1)} %fusion.87, f32[16,16,16]{2,1,0:T(8,128)S(1)} %bitcast.172), kind=kLoop, calls=%fused_computation.59 | loop fusion | flops 65536 | bytes 279552 | tf_op jit(solution)/shard_map/mul | solution.py:127
  75.2 2.4 %reshape.148 = f32[256,256,1,1]{1,0,2,3:T(8,128)S(1)} reshape(f32[16,16,16,16]{3,2,1,0:T(8,128)} %broadcast_multiply_fusion) | data formatting | bytes 524288 | tf_op jit(solution)/shard_map/mul | solution.py:127
  77.6 1.9 %fusion.34 = f32[2,4,256,128]{2,3,1,0:T(8,128)S(1)} fusion(f32[2,6,256,128]{2,3,1,0:T(8,128)S(1)} %convert_element_type.175, f32[2,4,256,1]{2,3,1,0:T(1,128)S(1)} %broadcast_in_dim.20, f32[2,4,256,127]{2,3,1,0:T(8,128)} %get-tuple-element.32, f32[2,4,256,127]{2,3,1,0:T(8,128)} %get-tuple-element.31, f32[2,4,256,1]{2,3,1,0:T(1,128)S(1)} %copy.120), kind=kLoop, calls=%fused_computation.43 | loop fusion | flops 1835008 | bytes 6291456 | tf_op jit(solution)/shard_map/sub | solution.py:30
  79.5 1.0 copy-done.1
  81.2 1.0 copy.121
  82.2 2.9 %fusion.14 = bf16[2,4,256,128]{2,3,1,0:T(8,128)(2,1)S(1)} fusion(bf16[2,4,256,128]{2,3,1,0:T(8,128)(2,1)} %copy-done.5, f32[2,4,256,128]{2,3,1,0:T(8,128)} %copy.126, f32[2,4,256,128]{2,3,1,0:T(8,128)} %copy-done.1, f32[2,6,256,128]{2,3,1,0:T(8,128)S(1)} %convert_element_type.175, f32[2,4,128]{2,1,0:T(4,128)S(1)} %copy-done.19, ...), kind=kOutput, calls=%fused_computation.19 | convolution fusion | flops 807403520 | bytes 4464640 | tf_op jit(solution)/shard_map/ij,fxjy->fxiy/dot_general | solution.py:160
  85.1 3.4 %collective-permute-start.4 = (bf16[2,1,256,128]{2,3,1,0:T(8,128)(2,1)S(1)}, bf16[2,1,256,128]{2,3,1,0:T(8,128)(2,1)S(1)}, u32[]{:S(2)}, u32[]{:S(2)}) collective-permute-start(bf16[2,1,256,128]{2,3,1,0:T(8,128)(2,1)S(1)} %get-tuple-element.39), channel_id=1, source_target_pairs={{0,4},{1,5},{2,6},{3,7},{4,8},{5,9},{6,10},{7,11},{8,12},{9,13},{1... | collective-permute-start | bytes 393224 | tf_op jit(solution)/shard_map/ppermute | solution.py:139
  88.5 6.1 %collective-permute-start.5 = (bf16[2,1,256,128]{2,3,1,0:T(8,128)(2,1)S(1)}, bf16[2,1,256,128]{2,3,1,0:T(8,128)(2,1)S(1)}, u32[]{:S(2)}, u32[]{:S(2)}) collective-permute-start(bf16[2,1,256,128]{2,3,1,0:T(8,128)(2,1)S(1)} %get-tuple-element.40), channel_id=1, source_target_pairs={{4,0},{5,1},{6,2},{7,3},{8,4},{9,5},{10,6},{11,7},{12,8},{13,9},{1... | collective-permute-start | bytes 393224 | tf_op jit(solution)/shard_map/ppermute | solution.py:140
  94.6 1.9 %collective-permute-start.6 = (bf16[2,4,256]{2,1,0:T(4,128)(2,1)S(1)}, bf16[2,4,256]{2,1,0:T(4,128)(2,1)S(1)}, u32[]{:S(2)}, u32[]{:S(2)}) collective-permute-start(bf16[2,4,256]{2,1,0:T(4,128)(2,1)S(1)} %bitcast.183), channel_id=1, source_target_pairs={{0,1},{1,2},{2,3},{4,5},{5,6},{6,7},{8,9},{9,10},{10,11},{12,13},{... | collective-permute-start | bytes 12296 | tf_op jit(solution)/shard_map/ppermute | solution.py:141
  96.6 1.3 collective-permute-start.7
  97.9 0.9 copy.122
  98.7 6.2 %all-to-all-start.1 = ((bf16[2,4,16,16,128]{4,3,1,0,2:T(8,128)(2,1)}), bf16[2,4,16,16,128]{4,3,1,0,2:T(8,128)(2,1)S(1)}, u32[]{:S(2)}, u32[]{:S(2)}) async-start(bf16[2,4,16,16,128]{4,3,1,0,2:T(8,128)(2,1)} %copy.122), calls=%async_computation.1 | async-start | bytes 1048576 | tf_op jit(solution)/shard_map/all_to_all | solution.py:132
  107.5 0.9 copy.131
  108.4 15.9 %all-to-all-done.1 = bf16[2,4,16,16,128]{4,3,1,0,2:T(8,128)(2,1)S(1)} async-done(((bf16[2,4,16,16,128]{4,3,1,0,2:T(8,128)(2,1)}), bf16[2,4,16,16,128]{4,3,1,0,2:T(8,128)(2,1)S(1)}, u32[]{:S(2)}, u32[]{:S(2)}) %all-to-all-start.1) | async-done | bytes 524320 | tf_op jit(solution)/shard_map/all_to_all | solution.py:132
  124.3 3.7 %all-to-all-start.3 = ((bf16[2,4,16,16,128]{4,3,1,0,2:T(8,128)(2,1)}), bf16[2,4,16,16,128]{4,3,1,0,2:T(8,128)(2,1)S(1)}, u32[]{:S(2)}, u32[]{:S(2)}) async-start(bf16[2,4,16,16,128]{4,3,1,0,2:T(8,128)(2,1)} %copy.131), calls=%async_computation.3 | async-start | bytes 1048576 | tf_op jit(solution)/shard_map/all_to_all | solution.py:132
  128.1 1.7 %fusion.95 = (f32[2,16,16,511]{3,2,1,0:T(8,128)}, f32[2,16,16,511]{3,2,1,0:T(8,128)}) fusion(f32[2,18,16,512]{3,2,1,0:T(8,128)S(1)} %get-tuple-element.33), kind=kLoop, calls=%fused_computation.153 | loop fusion | bytes 4186112 | tf_op jit(solution)/shard_map/slice | solution.py:28
  129.8 1.5 copy.158
  131.3 1.4 reshape.137
  132.7 3.6 %fusion.10 = f32[2,16,16,512]{3,2,1,0:T(8,128)S(1)} fusion(f32[2,16,16,512]{3,2,1,0:T(8,128)} %reshape.137, f32[2,18,16,512]{3,2,1,0:T(8,128)S(1)} %get-tuple-element.33, f32[2,16,16,511]{3,2,1,0:T(8,128)} %get-tuple-element.24, f32[2,16,16,511]{3,2,1,0:T(8,128)} %get-tuple-element.23, f32[2,16,512]{2,1,0:T(8,128)S(1)} %copy-done.9, ...), kind=kOutput, calls=%fused_computation.14 | convolution fusion | flops 53477376 | bytes 9048064 | tf_op jit(solution)/shard_map/ac,fxcy->fxay/dot_general | solution.py:178
  136.4 1.9 %collective-permute-start.2 = (f32[2,1,16,512]{3,2,1,0:T(8,128)S(1)}, f32[2,1,16,512]{3,2,1,0:T(8,128)S(1)}, u32[]{:S(2)}, u32[]{:S(2)}) collective-permute-start(f32[2,1,16,512]{3,2,1,0:T(8,128)S(1)} %get-tuple-element.27), channel_id=1, source_target_pairs={{16,0},{32,16},{48,32},{64,48},{80,64},{96,80},{112,96},{128,112},... | collective-permute-start | bytes 196616 | tf_op jit(solution)/shard_map/ppermute | solution.py:15
  138.3 2.8 %collective-permute-start.3 = (f32[2,1,16,512]{3,2,1,0:T(8,128)S(1)}, f32[2,1,16,512]{3,2,1,0:T(8,128)S(1)}, u32[]{:S(2)}, u32[]{:S(2)}) collective-permute-start(f32[2,1,16,512]{3,2,1,0:T(8,128)S(1)} %get-tuple-element.28), channel_id=1, source_target_pairs={{0,16},{16,32},{32,48},{48,64},{64,80},{80,96},{96,112},{112,128},... | collective-permute-start | bytes 196616 | tf_op jit(solution)/shard_map/ppermute | solution.py:14
  141.1 1.7 %fusion.96 = (f32[2,16,16,511]{3,2,1,0:T(8,128)}, f32[2,16,16,511]{3,2,1,0:T(8,128)}) fusion(f32[2,16,16,512]{3,2,1,0:T(8,128)S(1)} %fusion.10), kind=kLoop, calls=%fused_computation.154 | loop fusion | bytes 4186112 | tf_op jit(solution)/shard_map/slice | solution.py:28
  142.8 5.8 %all-to-all-done.3 = bf16[2,4,16,16,128]{4,3,1,0,2:T(8,128)(2,1)S(1)} async-done(((bf16[2,4,16,16,128]{4,3,1,0,2:T(8,128)(2,1)}), bf16[2,4,16,16,128]{4,3,1,0,2:T(8,128)(2,1)S(1)}, u32[]{:S(2)}, u32[]{:S(2)}) %all-to-all-start.3) | async-done | bytes 524320 | tf_op jit(solution)/shard_map/all_to_all | solution.py:132
  148.7 1.4 copy.133
  150.1 1.6 %reshape.141 = f32[2,16,16,512]{3,2,1,0:T(8,128)S(1)} reshape(f32[2,4,4,16,4,128]{5,4,3,2,1,0:T(4,128)} %copy.133) | data formatting | bytes 2097152 | tf_op jit(solution)/shard_map/convert_element_type | solution.py:176
  151.8 3.3 %fusion.8 = f32[2,16,16,512]{3,1,2,0:T(8,128)S(1)} fusion(f32[2,16,16,512]{3,2,1,0:T(8,128)S(1)} %fusion.10, f32[2,16,16,512]{3,2,1,0:T(8,128)S(1)} %reshape.141, f32[2,1,16,512]{3,2,1,0:T(8,128)S(1)} %collective-permute-done.3, f32[2,1,16,512]{3,2,1,0:T(8,128)S(1)} %collective-permute-done.2, f32[2,16,16,511]{3,2,1,0:T(8,128)} %get-tuple-element.26, ...), kind=kOutput, calls=%fused_computation.11 | convolution fusion | flops 54001664 | bytes 6026240 | tf_op jit(solution)/shard_map/ac,fxcy->fxay/dot_general | solution.py:178
  155.1 1.6 %copy.134 = f32[2,16,16,512]{3,2,1,0:T(8,128)} copy(f32[2,16,16,512]{3,1,2,0:T(8,128)S(1)} %fusion.8) | data formatting | bytes 2097152 | tf_op jit(solution)/shard_map/transpose | solution.py:180
  (119 shorter events, 10.1 us)
Async XLA Ops:
  1.3 25.4 %collective-permute-start = (bf16[2,1,16,512]{3,2,1,0:T(8,128)(2,1)S(1)}, bf16[2,1,16,512]{3,2,1,0:T(8,128)(2,1)S(1)}, u32[]{:S(2)}, u32[]{:S(2)}) collective-permute-start(bf16[2,1,16,512]{3,2,1,0:T(8,128)(2,1)S(1)} %get-tuple-element.41), channel_id=1, source_target_pairs={{0,16},{16,32},{32,48},{48,64},{64,80},{80,96},{96,112},{112,128},... | collective-permute-start | bytes 98312 | tf_op jit(solution)/shard_map/ppermute | solution.py:14
  3.3 23.4 %collective-permute-start.1 = (bf16[2,1,16,512]{3,2,1,0:T(8,128)(2,1)S(1)}, bf16[2,1,16,512]{3,2,1,0:T(8,128)(2,1)S(1)}, u32[]{:S(2)}, u32[]{:S(2)}) collective-permute-start(bf16[2,1,16,512]{3,2,1,0:T(8,128)(2,1)S(1)} %get-tuple-element.42), channel_id=1, source_target_pairs={{16,0},{32,16},{48,32},{64,48},{80,64},{96,80},{112,96},{128,112},... | collective-permute-start | bytes 98312 | tf_op jit(solution)/shard_map/ppermute | solution.py:15
  9.0 15.1 %copy-start.12 = (f32[1,16,16]{2,1,0:T(8,128)S(1)}, f32[1,16,16]{2,1,0:T(8,128)}, u32[]{:S(2)}) copy-start(f32[1,16,16]{2,1,0:T(8,128)} %param.15) | copy-start | bytes 3076
  10.2 30.5 %all-to-all-start.2 = ((bf16[16,2,4,16,128]{4,3,2,1,0:T(8,128)(2,1)}), bf16[16,2,4,16,128]{4,3,2,1,0:T(8,128)(2,1)S(1)}, u32[]{:S(2)}, u32[]{:S(2)}) async-start(bf16[16,2,4,16,128]{4,3,2,1,0:T(8,128)(2,1)} %bitcast.44), calls=%async_computation.2 | async-start | bytes 1048576 | tf_op jit(solution)/shard_map/all_to_all | solution.py:74
  27.7 16.7 %copy-start.15 = (s32[16,512]{1,0:T(8,128)S(1)}, s32[16,512]{1,0:T(8,128)}, u32[]{:S(2)}) copy-start(s32[16,512]{1,0:T(8,128)} %param.10) | copy-start | bytes 98308
  27.7 17.1 %copy-start.13 = (f32[2,3,8]{2,0,1:T(2,128)S(1)}, f32[2,3,8]{2,0,1:T(2,128)}, u32[]{:S(2)}) copy-start(f32[2,3,8]{2,0,1:T(2,128)} %param.12) | copy-start | bytes 580
  28.8 16.9 %copy-start.16 = (s32[3,16,16]{2,1,0:T(8,128)S(1)}, s32[3,16,16]{2,1,0:T(8,128)}, u32[]{:S(2)}) copy-start(s32[3,16,16]{2,1,0:T(8,128)} %param.14) | copy-start | bytes 9220
  40.7 7.1 %copy-start.3 = (bf16[16,2,4,16,128]{4,3,2,1,0:T(8,128)(2,1)}, bf16[16,2,4,16,128]{4,3,2,1,0:T(8,128)(2,1)S(1)}, u32[]{:S(2)}) copy-start(bf16[16,2,4,16,128]{4,3,2,1,0:T(8,128)(2,1)S(1)} %all-to-all-done.2) | copy-start | bytes 1572868
  40.7 28.5 %all-to-all-start = ((bf16[16,2,7,16,128]{4,3,2,1,0:T(8,128)(2,1)}), bf16[16,2,7,16,128]{4,3,2,1,0:T(8,128)(2,1)S(1)}, u32[]{:S(2)}, u32[]{:S(2)}) async-start(bf16[16,2,7,16,128]{4,3,2,1,0:T(8,128)(2,1)} %bitcast.20), calls=%async_computation | async-start | bytes 1835008 | tf_op jit(solution)/shard_map/all_to_all | solution.py:116
  47.8 5.1 %copy-start.14 = (f32[2,8]{1,0:T(2,128)S(1)}, f32[2,8]{1,0:T(2,128)}, u32[]{:S(2)}) copy-start(f32[2,8]{1,0:T(2,128)} %param.11) | copy-start | bytes 196
  54.0 0.6 copy-start.7
  69.4 0.9 copy-start.2
  77.6 2.9 %copy-start.10 = (bf16[3,256,256]{2,1,0:T(8,128)(2,1)S(1)}, bf16[3,256,256]{2,1,0:T(8,128)(2,1)}, u32[]{:S(2)}) copy-start(bf16[3,256,256]{2,1,0:T(8,128)(2,1)} %mul.583) | copy-start | bytes 1179652
  77.6 2.9 %copy-start.17 = (f32[2,4,3,128]{3,2,1,0:T(4,128)S(1)}, f32[2,4,3,128]{3,2,1,0:T(4,128)}, u32[]{:S(2)}) copy-start(f32[2,4,3,128]{3,2,1,0:T(4,128)} %fusion.84) | copy-start | bytes 36868
  77.6 2.9 %copy-start.21 = (bf16[3,256,256]{2,1,0:T(8,128)(2,1)S(1)}, bf16[3,256,256]{2,1,0:T(8,128)(2,1)}, u32[]{:S(2)}) copy-start(bf16[3,256,256]{2,1,0:T(8,128)(2,1)} %param.13) | copy-start | bytes 1179652
  79.5 1.0 copy-start.1
  80.5 1.7 %copy-start.19 = (f32[2,4,128]{2,1,0:T(4,128)S(1)}, f32[2,4,128]{2,1,0:T(4,128)}, u32[]{:S(2)}) copy-start(f32[2,4,128]{2,1,0:T(4,128)} %get-tuple-element.19) | copy-start | bytes 12292
  80.5 1.7 %copy-start.20 = (f32[2,4,128]{2,1,0:T(4,128)S(1)}, f32[2,4,128]{2,1,0:T(4,128)}, u32[]{:S(2)}) copy-start(f32[2,4,128]{2,1,0:T(4,128)} %get-tuple-element.20) | copy-start | bytes 12292
  81.1 1.0 copy-start.5
  82.2 15.7 %copy-start.6 = (bf16[2,4,256,128]{3,2,1,0:T(8,128)(2,1)S(1)}, bf16[2,4,256,128]{3,2,1,0:T(8,128)(2,1)}, u32[]{:S(2)}) copy-start(bf16[2,4,256,128]{3,2,1,0:T(8,128)(2,1)} %copy.121) | copy-start | bytes 1572868
  85.1 19.8 %collective-permute-start.4 = (bf16[2,1,256,128]{2,3,1,0:T(8,128)(2,1)S(1)}, bf16[2,1,256,128]{2,3,1,0:T(8,128)(2,1)S(1)}, u32[]{:S(2)}, u32[]{:S(2)}) collective-permute-start(bf16[2,1,256,128]{2,3,1,0:T(8,128)(2,1)S(1)} %get-tuple-element.39), channel_id=1, source_target_pairs={{0,4},{1,5},{2,6},{3,7},{4,8},{5,9},{6,10},{7,11},{8,12},{9,13},{1... | collective-permute-start | bytes 393224 | tf_op jit(solution)/shard_map/ppermute | solution.py:139
  88.5 16.4 %collective-permute-start.5 = (bf16[2,1,256,128]{2,3,1,0:T(8,128)(2,1)S(1)}, bf16[2,1,256,128]{2,3,1,0:T(8,128)(2,1)S(1)}, u32[]{:S(2)}, u32[]{:S(2)}) collective-permute-start(bf16[2,1,256,128]{2,3,1,0:T(8,128)(2,1)S(1)} %get-tuple-element.40), channel_id=1, source_target_pairs={{4,0},{5,1},{6,2},{7,3},{8,4},{9,5},{10,6},{11,7},{12,8},{13,9},{1... | collective-permute-start | bytes 393224 | tf_op jit(solution)/shard_map/ppermute | solution.py:140
  94.6 10.4 %collective-permute-start.6 = (bf16[2,4,256]{2,1,0:T(4,128)(2,1)S(1)}, bf16[2,4,256]{2,1,0:T(4,128)(2,1)S(1)}, u32[]{:S(2)}, u32[]{:S(2)}) collective-permute-start(bf16[2,4,256]{2,1,0:T(4,128)(2,1)S(1)} %bitcast.183), channel_id=1, source_target_pairs={{0,1},{1,2},{2,3},{4,5},{5,6},{6,7},{8,9},{9,10},{10,11},{12,13},{... | collective-permute-start | bytes 12296 | tf_op jit(solution)/shard_map/ppermute | solution.py:141
  96.6 8.5 %collective-permute-start.7 = (bf16[2,4,256]{2,1,0:T(4,128)(2,1)S(1)}, bf16[2,4,256]{2,1,0:T(4,128)(2,1)S(1)}, u32[]{:S(2)}, u32[]{:S(2)}) collective-permute-start(bf16[2,4,256]{2,1,0:T(4,128)(2,1)S(1)} %bitcast.184), channel_id=1, source_target_pairs={{1,0},{2,1},{3,2},{5,4},{6,5},{7,6},{9,8},{10,9},{11,10},{13,12},{... | collective-permute-start | bytes 12296 | tf_op jit(solution)/shard_map/ppermute | solution.py:142
  98.7 25.6 %all-to-all-start.1 = ((bf16[2,4,16,16,128]{4,3,1,0,2:T(8,128)(2,1)}), bf16[2,4,16,16,128]{4,3,1,0,2:T(8,128)(2,1)S(1)}, u32[]{:S(2)}, u32[]{:S(2)}) async-start(bf16[2,4,16,16,128]{4,3,1,0,2:T(8,128)(2,1)} %copy.122), calls=%async_computation.1 | async-start | bytes 1048576 | tf_op jit(solution)/shard_map/all_to_all | solution.py:132
  105.5 1.0 copy-start.11
  105.5 1.0 copy-start.18
  105.5 1.1 copy-start.22
  124.3 5.4 %copy-start.4 = (bf16[2,4,16,16,128]{4,3,1,0,2:T(8,128)(2,1)}, bf16[2,4,16,16,128]{4,3,1,0,2:T(8,128)(2,1)S(1)}, u32[]{:S(2)}) copy-start(bf16[2,4,16,16,128]{4,3,1,0,2:T(8,128)(2,1)S(1)} %all-to-all-done.1) | copy-start | bytes 1572868
  124.3 24.2 %all-to-all-start.3 = ((bf16[2,4,16,16,128]{4,3,1,0,2:T(8,128)(2,1)}), bf16[2,4,16,16,128]{4,3,1,0,2:T(8,128)(2,1)S(1)}, u32[]{:S(2)}, u32[]{:S(2)}) async-start(bf16[2,4,16,16,128]{4,3,1,0,2:T(8,128)(2,1)} %copy.131), calls=%async_computation.3 | async-start | bytes 1048576 | tf_op jit(solution)/shard_map/all_to_all | solution.py:132
  129.8 2.9 %copy-start = (bf16[2,16,16,512]{3,2,1,0:T(8,128)(2,1)S(1)}, bf16[2,16,16,512]{3,2,1,0:T(8,128)(2,1)}, u32[]{:S(2)}) copy-start(bf16[2,16,16,512]{3,2,1,0:T(8,128)(2,1)} %param.8) | copy-start | bytes 1572868
  129.8 2.9 %copy-start.8 = (f32[2,16,512]{2,1,0:T(8,128)S(1)}, f32[2,16,512]{2,1,0:T(8,128)}, u32[]{:S(2)}) copy-start(f32[2,16,512]{2,1,0:T(8,128)} %copy-done.7) | copy-start | bytes 196612
  129.8 2.9 %copy-start.9 = (f32[2,16,512]{2,1,0:T(8,128)S(1)}, f32[2,16,512]{2,1,0:T(8,128)}, u32[]{:S(2)}) copy-start(f32[2,16,512]{2,1,0:T(8,128)} %get-tuple-element.21) | copy-start | bytes 196612
  136.4 15.4 %collective-permute-start.2 = (f32[2,1,16,512]{3,2,1,0:T(8,128)S(1)}, f32[2,1,16,512]{3,2,1,0:T(8,128)S(1)}, u32[]{:S(2)}, u32[]{:S(2)}) collective-permute-start(f32[2,1,16,512]{3,2,1,0:T(8,128)S(1)} %get-tuple-element.27), channel_id=1, source_target_pairs={{16,0},{32,16},{48,32},{64,48},{80,64},{96,80},{112,96},{128,112},... | collective-permute-start | bytes 196616 | tf_op jit(solution)/shard_map/ppermute | solution.py:15
  138.3 13.5 %collective-permute-start.3 = (f32[2,1,16,512]{3,2,1,0:T(8,128)S(1)}, f32[2,1,16,512]{3,2,1,0:T(8,128)S(1)}, u32[]{:S(2)}, u32[]{:S(2)}) collective-permute-start(f32[2,1,16,512]{3,2,1,0:T(8,128)S(1)} %get-tuple-element.28), channel_id=1, source_target_pairs={{0,16},{16,32},{32,48},{48,64},{64,80},{80,96},{96,112},{112,128},... | collective-permute-start | bytes 196616 | tf_op jit(solution)/shard_map/ppermute | solution.py:14
where the time goes:
time: 158 us; the launch traced here: 157 us
  starting transfers between devices  50.3 us (32%)
  waiting for transfers between devices  44.3 us (28%)
  local copies, waits for them, and re-layouts  41.4 us (26%)
  matrix products  11 us (7%)
  other arithmetic  8.94 us (6%)
    all_to_all x2, waiting for transfers between devices, to_owner(): lax.all_to_all(mixed, 'modes', split_axis=2, concat_axis=2, tiled=True)  21.7 us
    all_to_all x1, starting transfers between devices, sweeps(): lax.all_to_all(rp, 'modes', split_axis=0, concat_axis=3, tiled=True)[0]  12.9 us
    all_to_all x1, waiting for transfers between devices, sweeps(): lax.all_to_all(rp, 'modes', split_axis=0, concat_axis=3, tiled=True)[0]  11.9 us
    all_to_all x1, waiting for transfers between devices, pack(): lax.all_to_all(full, 'modes', split_axis=0, concat_axis=3, tiled=True)[0]  10.6 us
    all_to_all x2, starting transfers between devices, to_owner(): lax.all_to_all(mixed, 'modes', split_axis=2, concat_axis=2, tiled=True)  9.9 us
    mul x2, local copies, waits for them, and re-layouts, sweeps(): shaped * block_mask[:, :, None, :, None].astype(jnp.bfloat16)  7.23 us
    dot_general x2, matrix products, sweeps(): jnp.einsum('ac,fxcy->fxay', own_inv, scaled, precision=lax.Precision.HIGH...  6.87 us
    ppermute x2, starting transfers between devices, ring_halo(): high = lax.ppermute(lax.slice_in_dim(block, 0, 1, axis=dim), axis, backward)  6.46 us
  transfers between devices with their start and end apart: 12, of which 4 were waited for; matrix products, arithmetic and copies ran while one was open for 24% of the time, Pallas kernels for 0%

commit v1 on v0

--- a/solution.py
+++ b/solution.py
@@ -131,7 +131,7 @@
         mixed = mixed.reshape(fields, rows_c, devs, modes_dev, LANES)
         back = lax.all_to_all(mixed, "modes", split_axis=2, concat_axis=2, tiled=True)
         back = back.reshape(fields, rows_c, row_chunks, col_chunks, modes_dev, LANES)
-        return back.transpose(0, 2, 1, 4, 3, 5).reshape(fields, rows, modes_dev, cols)
+        return back.transpose(0, 4, 2, 1, 3, 5).reshape(fields, modes_dev, rows, cols)
 
     coupled_owner = []
     for sweep in range(SWEEPS):
@@ -162,22 +162,25 @@
             )
             u_field = u_field + 0.6 * update
 
-    base_o = lookup(base_table, region)[:, :, None, :]
+    base_o = lookup(base_table, region)[:, None]
     inv_base_o = 1.0 / (4.0 * base_o)
-    rhs_o = rhs.transpose(0, 2, 1, 3).astype(jnp.float32)
+    rhs_o = rhs.astype(jnp.float32)
     own_inv = block_inverse[0]
-    pad_o = init_x.astype(jnp.float32)
-    u_o = pad_o[:, 1:-1]
-    zeros = jnp.zeros(u_o.shape[:-1], jnp.float32)
+    pad_o = init_x.transpose(0, 2, 1, 3).astype(jnp.float32)
+    u_o = pad_o[:, :, 1:-1]
+    zeros = jnp.zeros(u_o.shape[:-1] + (1,), jnp.float32)
     for sweep in range(SWEEPS):
         if sweep > 0:
-            pad_o = ring_halo(u_o, "space", 1)
-        lap_o = laplace_rows(pad_o, zeros, zeros)
+            pad_o = ring_halo(u_o, "space", 2)
+        center = pad_o[:, :, 1:-1]
+        right = jnp.concatenate([center[..., 1:], zeros], -1)
+        left = jnp.concatenate([zeros, center[..., :-1]], -1)
+        lap_o = 4.0 * center - pad_o[:, :, 2:] - pad_o[:, :, :-2] - right - left
         resid = rhs_o - base_o * lap_o - coupled_owner[sweep].astype(jnp.float32)
         scaled = resid * inv_base_o
-        update = jnp.einsum("ac,fxcy->fxay", own_inv, scaled, precision=lax.Precision.HIGHEST)
+        update = jnp.sum(own_inv[None, :, :, None, None] * scaled[:, None], axis=2)
         u_o = u_o + 0.6 * update
-    return u_o.transpose(0, 2, 1, 3)
+    return u_o
 
 
 def solution(mesh):

time: 158 us -> 167 us (1.057)
  waiting for transfers between devices: 44.3 us -> 22 us
  other arithmetic: 8.94 us -> 24.2 us
  local copies, waits for them, and re-layouts: 41.4 us -> 54.7 us
  starting transfers between devices: 50.3 us -> 58.5 us
  matrix products: 11 us -> 4.95 us
    all_to_all x1, waiting for transfers between devices: 11.9 us -> 0.01 us  [sweeps(): lax.all_to_all(rp, 'modes', split_axis=0, concat_axis=3, tiled=True)[0]]
    dot_general x2 -> x0, matrix products: 6.87 us -> none  [sweeps(): jnp.einsum('ac,fxcy->fxay', own_inv, scaled, precision=lax.Precision.HIGH...]
    all_to_all x1, waiting for transfers between devices: 10.6 us -> 4.59 us  [pack(): lax.all_to_all(full, 'modes', split_axis=0, concat_axis=3, tiled=True)[0]]
    all_to_all x1, starting transfers between devices: 3.64 us -> 9.63 us  [pack(): lax.all_to_all(full, 'modes', split_axis=0, concat_axis=3, tiled=True)[0]]
    mul x0 -> x2, other arithmetic: none -> 4.94 us  [sweeps(): scaled = resid * inv_base_o]
    reduce_sum x0 -> x2, other arithmetic: none -> 4.64 us  [sweeps(): update = jnp.sum(own_inv[None, :, :, None, None] * scaled[:, None], axis=2)]
    slice x10, local copies, waits for them, and re-layouts: 1.15 us -> 5.61 us  [lookup(): table[..., which, None, None] * (region == which).astype(jnp.float32)]
    all_to_all x2, waiting for transfers between devices: 21.7 us -> 17.4 us  [to_owner(): lax.all_to_all(mixed, 'modes', split_axis=2, concat_axis=2, tiled=True)]
  transfers between devices with their start and end apart: 12 -> 12, of which waited for: 4 -> 3; matrix products, arithmetic and copies ran while one was open for 24% -> 34% of each run, Pallas kernels for 0% -> 0%
where the time goes in v1:
time: 167 us; the launch traced here: 165 us
  starting transfers between devices  58.5 us (35%)
  local copies, waits for them, and re-layouts  54.7 us (33%)
  other arithmetic  24.2 us (14%)
  waiting for transfers between devices  22 us (13%)
  matrix products  4.95 us (3%)
    all_to_all x2, waiting for transfers between devices, to_owner(): lax.all_to_all(mixed, 'modes', split_axis=2, concat_axis=2, tiled=True)  17.4 us
    all_to_all x1, starting transfers between devices, sweeps(): lax.all_to_all(rp, 'modes', split_axis=0, concat_axis=3, tiled=True)[0]  13 us
    all_to_all x2, starting transfers between devices, to_owner(): lax.all_to_all(mixed, 'modes', split_axis=2, concat_axis=2, tiled=True)  11.9 us
    all_to_all x1, starting transfers between devices, pack(): lax.all_to_all(full, 'modes', split_axis=0, concat_axis=3, tiled=True)[0]  9.63 us
    mul x2, local copies, waits for them, and re-layouts, sweeps(): shaped * block_mask[:, :, None, :, None].astype(jnp.bfloat16)  7.3 us
    ppermute x2, starting transfers between devices, ring_halo(): high = lax.ppermute(lax.slice_in_dim(block, 0, 1, axis=dim), axis, backward)  6.59 us
    ppermute x1, starting transfers between devices, sweeps(): high = lax.ppermute(u_field[:, :1], flat, up)  6.17 us
    convert_element_type x4, local copies, waits for them, and re-layouts, sweeps(): resid = rhs_o - base_o * lap_o - coupled_owner[sweep].astype(jnp.float32)  5.86 us
  transfers between devices with their start and end apart: 12, of which 3 were waited for; matrix products, arithmetic and copies ran while one was open for 34% of the time, Pallas kernels for 0%

profile of v1, /device:TPU:24, one launch (start us, length us, event | category | flops | bytes accessed | tf_op | source)
XLA Modules:
  0.0 165.3 jit_solution(4835968011273194134)
XLA Ops:
  0.0 1.1 fusion.63
  1.1 1.9 %collective-permute-start = (bf16[2,1,16,512]{3,1,2,0:T(2,128)(2,1)S(1)}, bf16[2,1,16,512]{3,1,2,0:T(2,128)(2,1)S(1)}, u32[]{:S(2)}, u32[]{:S(2)}) collective-permute-start(bf16[2,1,16,512]{3,1,2,0:T(2,128)(2,1)S(1)} %get-tuple-element.39), channel_id=1, source_target_pairs={{0,16},{16,32},{32,48},{48,64},{64,80},{80,96},{96,112},{112,128},... | collective-permute-start | bytes 98312 | tf_op jit(solution)/shard_map/ppermute | solution.py:14
  3.1 4.7 %collective-permute-start.1 = (bf16[2,1,16,512]{3,1,2,0:T(2,128)(2,1)S(1)}, bf16[2,1,16,512]{3,1,2,0:T(2,128)(2,1)}, u32[]{:S(2)}, u32[]{:S(2)}) collective-permute-start(bf16[2,1,16,512]{3,1,2,0:T(2,128)(2,1)S(1)} %get-tuple-element.40), channel_id=1, source_target_pairs={{16,0},{32,16},{48,32},{64,48},{80,64},{96,80},{112,96},{128,112},... | collective-permute-start | bytes 98312 | tf_op jit(solution)/shard_map/ppermute | solution.py:15
  7.8 1.2 reshape.136
  8.9 1.1 copy.145
  10.1 13.0 %all-to-all-start.2 = ((bf16[16,2,4,16,128]{4,3,2,1,0:T(8,128)(2,1)}), bf16[16,2,4,16,128]{4,3,2,1,0:T(8,128)(2,1)S(1)}, u32[]{:S(2)}, u32[]{:S(2)}) async-start(bf16[16,2,4,16,128]{4,3,2,1,0:T(8,128)(2,1)} %bitcast.41), calls=%async_computation.2 | async-start | bytes 1048576 | tf_op jit(solution)/shard_map/all_to_all | solution.py:74
  30.8 2.1 %convert_bitcast_fusion = (f32[2,16,18,512]{3,2,1,0:T(8,128)S(1)}, bf16[2,18,16,512]{3,1,2,0:T(8,128)(2,1)}) fusion(bf16[2,1,16,512]{3,1,2,0:T(2,128)(2,1)} %collective-permute-done.1, bf16[2,16,16,512]{3,1,2,0:T(8,128)(2,1)S(1)} %bitcast.135, bf16[2,1,16,512]{3,1,2,0:T(2,128)(2,1)S(1)} %collective-permute-done), kind=kLoop, calls=%fused_computation.6 | loop fusion | flops 2064384 | bytes 2359296 | tf_op jit(solution)/shard_map/convert_element_type | solution.py:169
  32.9 3.0 %slice.206 = bf16[2,4,16,512]{3,1,2,0:T(4,128)(2,1)S(1)} slice(bf16[2,18,16,512]{3,1,2,0:T(8,128)(2,1)} %get-tuple-element.34), slice={[0:2:1], [0:16:4], [0:16:1], [0:512:1]} | slice | bytes 262144 | tf_op jit(solution)/shard_map/slice | solution.py:97
  35.9 3.0 %slice.207 = bf16[2,4,16,512]{3,1,2,0:T(4,128)(2,1)S(1)} slice(bf16[2,18,16,512]{3,1,2,0:T(8,128)(2,1)} %get-tuple-element.34), slice={[0:2:1], [5:18:4], [0:16:1], [0:512:1]} | slice | bytes 262144 | tf_op jit(solution)/shard_map/slice | solution.py:99
  39.9 1.2 copy.137
  41.0 9.6 %all-to-all-start = ((bf16[16,2,7,16,128]{4,3,2,1,0:T(8,128)(2,1)}), bf16[16,2,7,16,128]{4,3,2,1,0:T(8,128)(2,1)S(1)}, u32[]{:S(2)}, u32[]{:S(2)}) async-start(bf16[16,2,7,16,128]{4,3,2,1,0:T(8,128)(2,1)} %bitcast.20), calls=%async_computation | async-start | bytes 1835008 | tf_op jit(solution)/shard_map/all_to_all | solution.py:116
  56.0 2.1 %mul.604 = bf16[3,16,16,16,16]{4,3,2,1,0:T(8,128)(2,1)} broadcast(bf16[3,16,16]{2,1,0:T(8,128)(2,1)S(1)} %convert_element_type.179), dimensions={0,1,3} | broadcast | bytes 394752 | tf_op jit(solution)/shard_map/mul | solution.py:39
  58.2 5.2 %mul.605 = bf16[3,256,256]{2,1,0:T(8,128)(2,1)} reshape(bf16[3,16,16,16,16]{4,3,2,1,0:T(8,128)(2,1)} %mul.604) | data formatting | bytes 786432 | tf_op jit(solution)/shard_map/mul | solution.py:39
  65.2 1.0 multiply_add_fusion.2
  66.1 1.4 fusion.53
  67.5 1.8 %fusion.56 = (f32[2,16,16,511]{3,2,1,0:T(8,128)}, f32[2,16,16,511]{3,2,1,0:T(8,128)}) fusion(f32[2,16,18,512]{3,2,1,0:T(8,128)S(1)} %get-tuple-element.33), kind=kLoop, calls=%fused_computation.121 | loop fusion | bytes 4186112 | tf_op jit(solution)/shard_map/slice | solution.py:176
  69.5 1.4 copy.147
  70.8 4.6 %all-to-all-done = bf16[16,2,7,16,128]{4,3,2,1,0:T(8,128)(2,1)S(1)} async-done(((bf16[16,2,7,16,128]{4,3,2,1,0:T(8,128)(2,1)}), bf16[16,2,7,16,128]{4,3,2,1,0:T(8,128)(2,1)S(1)}, u32[]{:S(2)}, u32[]{:S(2)}) %all-to-all-start) | async-done | bytes 917536 | tf_op jit(solution)/shard_map/all_to_all | solution.py:116
  75.7 0.9 copy-done.4
  77.8 1.5 fusion.60
  79.4 1.3 convert_element_type.175
  81.9 1.6 broadcast_multiply_fusion
  83.5 2.4 %reshape.150 = f32[256,256,1,1]{1,0,2,3:T(8,128)S(1)} reshape(f32[16,16,16,16]{3,2,1,0:T(8,128)} %broadcast_multiply_fusion) | data formatting | bytes 524288 | tf_op jit(solution)/shard_map/mul | solution.py:127
  86.0 1.9 %fusion.26 = f32[2,4,256,128]{2,3,1,0:T(8,128)S(1)} fusion(f32[2,6,256,128]{2,3,1,0:T(8,128)S(1)} %convert_element_type.175, f32[2,4,256,1]{2,3,1,0:T(1,128)S(1)} %broadcast_in_dim.20, f32[2,4,256,127]{2,3,1,0:T(8,128)} %get-tuple-element.32, f32[2,4,256,127]{2,3,1,0:T(8,128)} %get-tuple-element.31, f32[2,4,256,1]{2,3,1,0:T(1,128)S(1)} %copy.141), kind=kLoop, calls=%fused_computation.40 | loop fusion | flops 1835008 | bytes 6291456 | tf_op jit(solution)/shard_map/sub | solution.py:30
  87.8 1.0 copy-done.2
  88.8 1.4 fusion.13
  90.3 2.0 %copy.142 = bf16[2,4,256,128]{3,2,1,0:T(8,128)(2,1)} copy(bf16[2,4,256,128]{2,3,1,0:T(8,128)(2,1)} %fusion.13) | data formatting | bytes 1048576 | tf_op jit(solution)/shard_map/convert_element_type | solution.py:155
  92.3 2.9 %fusion.9 = bf16[2,4,256,128]{2,3,1,0:T(8,128)(2,1)S(1)} fusion(bf16[2,4,256,128]{2,3,1,0:T(8,128)(2,1)} %fusion.13, f32[2,4,256,128]{2,3,1,0:T(8,128)} %copy.147, f32[2,4,256,128]{2,3,1,0:T(8,128)} %copy-done.2, f32[2,6,256,128]{2,3,1,0:T(8,128)S(1)} %convert_element_type.175, f32[2,4,128]{2,1,0:T(4,128)S(1)} %copy-done.34, ...), kind=kOutput, calls=%fused_computation.15 | convolution fusion | flops 807403520 | bytes 4464640 | tf_op jit(solution)/shard_map/ij,fxjy->fxiy/dot_general | solution.py:160
  95.2 3.3 %collective-permute-start.4 = (bf16[2,1,256,128]{2,3,1,0:T(8,128)(2,1)S(1)}, bf16[2,1,256,128]{2,3,1,0:T(8,128)(2,1)S(1)}, u32[]{:S(2)}, u32[]{:S(2)}) collective-permute-start(bf16[2,1,256,128]{2,3,1,0:T(8,128)(2,1)S(1)} %get-tuple-element.37), channel_id=1, source_target_pairs={{0,4},{1,5},{2,6},{3,7},{4,8},{5,9},{6,10},{7,11},{8,12},{9,13},{1... | collective-permute-start | bytes 393224 | tf_op jit(solution)/shard_map/ppermute | solution.py:139
  98.6 6.2 %collective-permute-start.5 = (bf16[2,1,256,128]{2,3,1,0:T(8,128)(2,1)S(1)}, bf16[2,1,256,128]{2,3,1,0:T(8,128)(2,1)S(1)}, u32[]{:S(2)}, u32[]{:S(2)}) collective-permute-start(bf16[2,1,256,128]{2,3,1,0:T(8,128)(2,1)S(1)} %get-tuple-element.38), channel_id=1, source_target_pairs={{4,0},{5,1},{6,2},{7,3},{8,4},{9,5},{10,6},{11,7},{12,8},{13,9},{1... | collective-permute-start | bytes 393224 | tf_op jit(solution)/shard_map/ppermute | solution.py:140
  104.8 2.3 %collective-permute-start.6 = (bf16[2,4,256]{2,1,0:T(4,128)(2,1)S(1)}, bf16[2,4,256]{2,1,0:T(4,128)(2,1)S(1)}, u32[]{:S(2)}, u32[]{:S(2)}) collective-permute-start(bf16[2,4,256]{2,1,0:T(4,128)(2,1)S(1)} %bitcast.156), channel_id=1, source_target_pairs={{0,1},{1,2},{2,3},{4,5},{5,6},{6,7},{8,9},{9,10},{10,11},{12,13},{... | collective-permute-start | bytes 12296 | tf_op jit(solution)/shard_map/ppermute | solution.py:141
  107.1 1.3 collective-permute-start.7
  109.2 7.4 %all-to-all-start.1 = ((bf16[2,4,16,16,128]{4,3,1,0,2:T(8,128)(2,1)}), bf16[2,4,16,16,128]{4,3,1,0,2:T(8,128)(2,1)S(1)}, u32[]{:S(2)}, u32[]{:S(2)}) async-start(bf16[2,4,16,16,128]{4,3,1,0,2:T(8,128)(2,1)} %copy.143), calls=%async_computation.1 | async-start | bytes 1048576 | tf_op jit(solution)/shard_map/all_to_all | solution.py:132
  120.2 14.7 %all-to-all-done.1 = bf16[2,4,16,16,128]{4,3,1,0,2:T(8,128)(2,1)S(1)} async-done(((bf16[2,4,16,16,128]{4,3,1,0,2:T(8,128)(2,1)}), bf16[2,4,16,16,128]{4,3,1,0,2:T(8,128)(2,1)S(1)}, u32[]{:S(2)}, u32[]{:S(2)}) %all-to-all-start.1) | async-done | bytes 524320 | tf_op jit(solution)/shard_map/all_to_all | solution.py:132
  134.8 4.5 %all-to-all-start.3 = ((bf16[2,4,16,16,128]{4,3,1,0,2:T(8,128)(2,1)}), bf16[2,4,16,16,128]{4,3,1,0,2:T(8,128)(2,1)}, u32[]{:S(2)}, u32[]{:S(2)}) async-start(bf16[2,4,16,16,128]{4,3,1,0,2:T(8,128)(2,1)} %copy.152), calls=%async_computation.3 | async-start | bytes 1048576 | tf_op jit(solution)/shard_map/all_to_all | solution.py:132
  139.3 1.4 copy.169
  140.7 1.6 reshape.140
  142.4 2.3 %fusion.15 = f32[2,16,16,512]{3,2,1,0:T(8,128)S(1)} fusion(f32[2,16,16,512]{3,2,1,0:T(8,128)S(1)} %reshape.140, bf16[2,16,16,512]{3,2,1,0:T(8,128)(2,1)S(1)} %copy-done.1, f32[2,16,18,512]{3,2,1,0:T(8,128)S(1)} %get-tuple-element.33, f32[2,16,16,511]{3,2,1,0:T(8,128)} %get-tuple-element.24, f32[2,16,16,511]{3,2,1,0:T(8,128)} %get-tuple-element.23, ...), kind=kLoop, calls=%fused_computation.23 | loop fusion | flops 2621440 | bytes 7991296 | tf_op jit(solution)/shard_map/mul | solution.py:180
  144.7 2.3 %multiply_reduce_fusion.1 = f32[2,16,16,512]{3,2,1,0:T(8,128)S(1)} fusion(f32[2,16,16,512]{3,2,1,0:T(8,128)S(1)} %fusion.15, f32[16,16]{1,0:T(8,128)S(1)} %bitcast.146), kind=kLoop, calls=%fused_computation.1 | loop fusion | flops 8126464 | bytes 2098176 | tf_op jit(solution)/shard_map/reduce_sum | solution.py:181
  147.5 1.9 %collective-permute-start.2 = (f32[2,16,1,512]{3,2,1,0:T(1,128)S(1)}, f32[2,16,1,512]{3,2,1,0:T(1,128)S(1)}, u32[]{:S(2)}, u32[]{:S(2)}) collective-permute-start(f32[2,16,1,512]{3,2,1,0:T(1,128)S(1)} %get-tuple-element.27), channel_id=1, source_target_pairs={{16,0},{32,16},{48,32},{64,48},{80,64},{96,80},{112,96},{128,112},... | collective-permute-start | bytes 196616 | tf_op jit(solution)/shard_map/ppermute | solution.py:15
  149.4 2.4 %collective-permute-start.3 = (f32[2,16,1,512]{3,2,1,0:T(1,128)S(1)}, f32[2,16,1,512]{3,2,1,0:T(1,128)S(1)}, u32[]{:S(2)}, u32[]{:S(2)}) collective-permute-start(f32[2,16,1,512]{3,2,1,0:T(1,128)S(1)} %get-tuple-element.28), channel_id=1, source_target_pairs={{0,16},{16,32},{32,48},{48,64},{64,80},{80,96},{96,112},{112,128},... | collective-permute-start | bytes 196616 | tf_op jit(solution)/shard_map/ppermute | solution.py:14
  151.8 1.7 %fusion.57 = (f32[2,16,16,511]{3,2,1,0:T(8,128)}, f32[2,16,16,511]{3,2,1,0:T(8,128)}) fusion(f32[2,16,16,512]{3,2,1,0:T(8,128)S(1)} %multiply_add_fusion.1), kind=kLoop, calls=%fused_computation.122 | loop fusion | bytes 4186112 | tf_op jit(solution)/shard_map/slice | solution.py:176
  153.5 2.8 %all-to-all-done.3 = bf16[2,4,16,16,128]{4,3,1,0,2:T(8,128)(2,1)} async-done(((bf16[2,4,16,16,128]{4,3,1,0,2:T(8,128)(2,1)}), bf16[2,4,16,16,128]{4,3,1,0,2:T(8,128)(2,1)}, u32[]{:S(2)}, u32[]{:S(2)}) %all-to-all-start.3) | async-done | bytes 524320 | tf_op jit(solution)/shard_map/all_to_all | solution.py:132
  156.3 1.4 copy.168
  157.7 1.4 reshape.144
  159.1 2.6 %fusion.17 = f32[2,16,16,512]{3,2,1,0:T(8,128)S(1)} fusion(f32[2,16,16,512]{3,2,1,0:T(8,128)} %reshape.144, bf16[2,16,16,512]{3,2,1,0:T(8,128)(2,1)S(1)} %copy-done.1, f32[2,16,16,512]{3,2,1,0:T(8,128)S(1)} %multiply_add_fusion.1, f32[2,16,1,512]{3,2,1,0:T(1,128)S(1)} %collective-permute-done.3, f32[2,16,1,512]{3,2,1,0:T(1,128)S(1)} %collective-permute-done.2, ...), kind=kLoop, calls=%fused_computation.25 | loop fusion | flops 3145728 | bytes 6025216 | tf_op jit(solution)/shard_map/mul | solution.py:180
  161.8 2.3 %multiply_reduce_fusion = f32[2,16,16,512]{3,2,1,0:T(8,128)S(1)} fusion(f32[2,16,16,512]{3,2,1,0:T(8,128)S(1)} %fusion.17, f32[16,16]{1,0:T(8,128)S(1)} %bitcast.147), kind=kLoop, calls=%fused_computation | loop fusion | flops 8126464 | bytes 2098176 | tf_op jit(solution)/shard_map/reduce_sum | solution.py:181
  164.1 1.2 multiply_add_fusion
  (150 shorter events, 23.0 us)
Async XLA Ops:
  1.1 29.6 %collective-permute-start = (bf16[2,1,16,512]{3,1,2,0:T(2,128)(2,1)S(1)}, bf16[2,1,16,512]{3,1,2,0:T(2,128)(2,1)S(1)}, u32[]{:S(2)}, u32[]{:S(2)}) collective-permute-start(bf16[2,1,16,512]{3,1,2,0:T(2,128)(2,1)S(1)} %get-tuple-element.39), channel_id=1, source_target_pairs={{0,16},{16,32},{32,48},{48,64},{64,80},{80,96},{96,112},{112,128},... | collective-permute-start | bytes 98312 | tf_op jit(solution)/shard_map/ppermute | solution.py:14
  3.1 20.0 %copy-start.3 = (bf16[2,16,16,512]{3,2,1,0:T(8,128)(2,1)S(1)}, bf16[2,16,16,512]{3,2,1,0:T(8,128)(2,1)}, u32[]{:S(2)}) copy-start(bf16[2,16,16,512]{3,2,1,0:T(8,128)(2,1)} %param.9) | copy-start | bytes 1572868
  3.1 27.7 %collective-permute-start.1 = (bf16[2,1,16,512]{3,1,2,0:T(2,128)(2,1)S(1)}, bf16[2,1,16,512]{3,1,2,0:T(2,128)(2,1)}, u32[]{:S(2)}, u32[]{:S(2)}) collective-permute-start(bf16[2,1,16,512]{3,1,2,0:T(2,128)(2,1)S(1)} %get-tuple-element.40), channel_id=1, source_target_pairs={{16,0},{32,16},{48,32},{64,48},{80,64},{96,80},{112,96},{128,112},... | collective-permute-start | bytes 98312 | tf_op jit(solution)/shard_map/ppermute | solution.py:15
  8.9 15.3 %copy-start.18 = (f32[1,16,16]{2,1,0:T(8,128)S(1)}, f32[1,16,16]{2,1,0:T(8,128)}, u32[]{:S(2)}) copy-start(f32[1,16,16]{2,1,0:T(8,128)} %param.15) | copy-start | bytes 3076
  10.1 16.1 %copy-start.31 = (s32[16,512]{1,0:T(8,128)S(1)}, s32[16,512]{1,0:T(8,128)}, u32[]{:S(2)}) copy-start(s32[16,512]{1,0:T(8,128)} %param.10) | copy-start | bytes 98308
  10.1 30.9 %all-to-all-start.2 = ((bf16[16,2,4,16,128]{4,3,2,1,0:T(8,128)(2,1)}), bf16[16,2,4,16,128]{4,3,2,1,0:T(8,128)(2,1)S(1)}, u32[]{:S(2)}, u32[]{:S(2)}) async-start(bf16[16,2,4,16,128]{4,3,2,1,0:T(8,128)(2,1)} %bitcast.41), calls=%async_computation.2 | async-start | bytes 1048576 | tf_op jit(solution)/shard_map/all_to_all | solution.py:74
  26.9 6.0 %copy-start.20 = (f32[16,512]{1,0:T(8,128)}, f32[16,512]{1,0:T(8,128)S(1)}, u32[]{:S(2)}) copy-start(f32[16,512]{1,0:T(8,128)S(1)} %get-tuple-element.43) | copy-start | bytes 98308
  26.9 6.0 %copy-start.22 = (f32[16,512]{1,0:T(8,128)}, f32[16,512]{1,0:T(8,128)S(1)}, u32[]{:S(2)}) copy-start(f32[16,512]{1,0:T(8,128)S(1)} %get-tuple-element.44) | copy-start | bytes 98308
  26.9 6.0 %copy-start.24 = (f32[16,512]{1,0:T(8,128)}, f32[16,512]{1,0:T(8,128)S(1)}, u32[]{:S(2)}) copy-start(f32[16,512]{1,0:T(8,128)S(1)} %get-tuple-element.45) | copy-start | bytes 98308
  26.9 6.0 %copy-start.26 = (f32[16,512]{1,0:T(8,128)}, f32[16,512]{1,0:T(8,128)S(1)}, u32[]{:S(2)}) copy-start(f32[16,512]{1,0:T(8,128)S(1)} %get-tuple-element.49) | copy-start | bytes 98308
  26.9 6.0 %copy-start.28 = (f32[16,512]{1,0:T(8,128)}, f32[16,512]{1,0:T(8,128)S(1)}, u32[]{:S(2)}) copy-start(f32[16,512]{1,0:T(8,128)S(1)} %get-tuple-element.50) | copy-start | bytes 98308
  39.8 10.8 %copy-start.19 = (f32[2,3,8]{2,0,1:T(2,128)S(1)}, f32[2,3,8]{2,0,1:T(2,128)}, u32[]{:S(2)}) copy-start(f32[2,3,8]{2,0,1:T(2,128)} %param.12) | copy-start | bytes 580
  39.8 16.2 %copy-start.32 = (s32[3,16,16]{2,1,0:T(8,128)S(1)}, s32[3,16,16]{2,1,0:T(8,128)}, u32[]{:S(2)}) copy-start(s32[3,16,16]{2,1,0:T(8,128)} %param.14) | copy-start | bytes 9220
  41.0 17.1 %copy-start.7 = (bf16[16,2,4,16,128]{4,3,2,1,0:T(8,128)(2,1)}, bf16[16,2,4,16,128]{4,3,2,1,0:T(8,128)(2,1)S(1)}, u32[]{:S(2)}) copy-start(bf16[16,2,4,16,128]{4,3,2,1,0:T(8,128)(2,1)S(1)} %all-to-all-done.2) | copy-start | bytes 1572868
  41.0 34.4 %all-to-all-start = ((bf16[16,2,7,16,128]{4,3,2,1,0:T(8,128)(2,1)}), bf16[16,2,7,16,128]{4,3,2,1,0:T(8,128)(2,1)S(1)}, u32[]{:S(2)}, u32[]{:S(2)}) async-start(bf16[16,2,7,16,128]{4,3,2,1,0:T(8,128)(2,1)} %bitcast.20), calls=%async_computation | async-start | bytes 1835008 | tf_op jit(solution)/shard_map/all_to_all | solution.py:116
  58.1 5.3 %copy-start.30 = (f32[2,8]{1,0:T(2,128)S(1)}, f32[2,8]{1,0:T(2,128)}, u32[]{:S(2)}) copy-start(f32[2,8]{1,0:T(2,128)} %param.11) | copy-start | bytes 196
  58.1 5.6 %copy-start.15 = (f32[16,512]{1,0:T(8,128)S(1)}, f32[16,512]{1,0:T(8,128)}, u32[]{:S(2)}) copy-start(f32[16,512]{1,0:T(8,128)} %get-tuple-element.46) | copy-start | bytes 98308
  58.1 5.6 %copy-start.16 = (f32[16,512]{1,0:T(8,128)S(1)}, f32[16,512]{1,0:T(8,128)}, u32[]{:S(2)}) copy-start(f32[16,512]{1,0:T(8,128)} %get-tuple-element.47) | copy-start | bytes 98308
  58.1 5.6 %copy-start.17 = (f32[16,512]{1,0:T(8,128)S(1)}, f32[16,512]{1,0:T(8,128)}, u32[]{:S(2)}) copy-start(f32[16,512]{1,0:T(8,128)} %get-tuple-element.48) | copy-start | bytes 98308
  58.1 5.6 %copy-start.21 = (f32[16,512]{1,0:T(8,128)S(1)}, f32[16,512]{1,0:T(8,128)}, u32[]{:S(2)}) copy-start(f32[16,512]{1,0:T(8,128)} %copy-done.20) | copy-start | bytes 98308
  58.1 5.6 %copy-start.23 = (f32[16,512]{1,0:T(8,128)S(1)}, f32[16,512]{1,0:T(8,128)}, u32[]{:S(2)}) copy-start(f32[16,512]{1,0:T(8,128)} %copy-done.22) | copy-start | bytes 98308
  58.1 5.6 %copy-start.25 = (f32[16,512]{1,0:T(8,128)S(1)}, f32[16,512]{1,0:T(8,128)}, u32[]{:S(2)}) copy-start(f32[16,512]{1,0:T(8,128)} %copy-done.24) | copy-start | bytes 98308
  58.2 5.6 %copy-start.27 = (f32[16,512]{1,0:T(8,128)S(1)}, f32[16,512]{1,0:T(8,128)}, u32[]{:S(2)}) copy-start(f32[16,512]{1,0:T(8,128)} %copy-done.26) | copy-start | bytes 98308
  58.2 5.6 %copy-start.29 = (f32[16,512]{1,0:T(8,128)S(1)}, f32[16,512]{1,0:T(8,128)}, u32[]{:S(2)}) copy-start(f32[16,512]{1,0:T(8,128)} %copy-done.28) | copy-start | bytes 98308
  64.5 3.0 %copy-start.10 = (f32[2,16,512]{2,1,0:T(8,128)}, f32[2,16,512]{2,1,0:T(8,128)S(1)}, u32[]{:S(2)}) copy-start(f32[2,16,512]{2,1,0:T(8,128)S(1)} %get-tuple-element.22) | copy-start | bytes 196612
  67.5 1.9 %copy-start.8 = (bf16[16,2,4,16,128]{4,3,2,1,0:T(8,128)(2,1)S(1)}, bf16[16,2,4,16,128]{4,3,2,1,0:T(8,128)(2,1)}, u32[]{:S(2)}) copy-start(bf16[16,2,4,16,128]{4,3,2,1,0:T(8,128)(2,1)} %copy-done.7) | copy-start | bytes 1572868
  85.9 2.9 %copy-start.13 = (bf16[3,256,256]{2,1,0:T(8,128)(2,1)S(1)}, bf16[3,256,256]{2,1,0:T(8,128)(2,1)}, u32[]{:S(2)}) copy-start(bf16[3,256,256]{2,1,0:T(8,128)(2,1)} %mul.605) | copy-start | bytes 1179652
  85.9 2.9 %copy-start.33 = (f32[2,4,3,128]{3,2,1,0:T(4,128)S(1)}, f32[2,4,3,128]{3,2,1,0:T(4,128)}, u32[]{:S(2)}) copy-start(f32[2,4,3,128]{3,2,1,0:T(4,128)} %fusion.53) | copy-start | bytes 36868
  85.9 2.9 %copy-start.36 = (bf16[3,256,256]{2,1,0:T(8,128)(2,1)S(1)}, bf16[3,256,256]{2,1,0:T(8,128)(2,1)}, u32[]{:S(2)}) copy-start(bf16[3,256,256]{2,1,0:T(8,128)(2,1)} %param.13) | copy-start | bytes 1179652
  87.8 1.0 copy-start.2
  88.8 3.5 %copy-start.34 = (f32[2,4,128]{2,1,0:T(4,128)S(1)}, f32[2,4,128]{2,1,0:T(4,128)}, u32[]{:S(2)}) copy-start(f32[2,4,128]{2,1,0:T(4,128)} %get-tuple-element.19) | copy-start | bytes 12292
  88.8 3.5 %copy-start.35 = (f32[2,4,128]{2,1,0:T(4,128)S(1)}, f32[2,4,128]{2,1,0:T(4,128)}, u32[]{:S(2)}) copy-start(f32[2,4,128]{2,1,0:T(4,128)} %get-tuple-element.20) | copy-start | bytes 12292
  92.3 16.0 %copy-start.9 = (bf16[2,4,256,128]{3,2,1,0:T(8,128)(2,1)S(1)}, bf16[2,4,256,128]{3,2,1,0:T(8,128)(2,1)}, u32[]{:S(2)}) copy-start(bf16[2,4,256,128]{3,2,1,0:T(8,128)(2,1)} %copy.142) | copy-start | bytes 1572868
  95.2 9.5 %copy-start.5 = (bf16[2,4,256,128]{2,3,1,0:T(8,128)(2,1)}, bf16[2,4,256,128]{2,3,1,0:T(8,128)(2,1)S(1)}, u32[]{:S(2)}) copy-start(bf16[2,4,256,128]{2,3,1,0:T(8,128)(2,1)S(1)} %fusion.9) | copy-start | bytes 1572868
  95.2 21.4 %collective-permute-start.4 = (bf16[2,1,256,128]{2,3,1,0:T(8,128)(2,1)S(1)}, bf16[2,1,256,128]{2,3,1,0:T(8,128)(2,1)S(1)}, u32[]{:S(2)}, u32[]{:S(2)}) collective-permute-start(bf16[2,1,256,128]{2,3,1,0:T(8,128)(2,1)S(1)} %get-tuple-element.37), channel_id=1, source_target_pairs={{0,4},{1,5},{2,6},{3,7},{4,8},{5,9},{6,10},{7,11},{8,12},{9,13},{1... | collective-permute-start | bytes 393224 | tf_op jit(solution)/shard_map/ppermute | solution.py:139
  98.6 18.1 %collective-permute-start.5 = (bf16[2,1,256,128]{2,3,1,0:T(8,128)(2,1)S(1)}, bf16[2,1,256,128]{2,3,1,0:T(8,128)(2,1)S(1)}, u32[]{:S(2)}, u32[]{:S(2)}) collective-permute-start(bf16[2,1,256,128]{2,3,1,0:T(8,128)(2,1)S(1)} %get-tuple-element.38), channel_id=1, source_target_pairs={{4,0},{5,1},{6,2},{7,3},{8,4},{9,5},{10,6},{11,7},{12,8},{13,9},{1... | collective-permute-start | bytes 393224 | tf_op jit(solution)/shard_map/ppermute | solution.py:140
  104.8 11.9 %copy-start.6 = (bf16[2,4,256,128]{2,3,1,0:T(8,128)(2,1)S(1)}, bf16[2,4,256,128]{2,3,1,0:T(8,128)(2,1)}, u32[]{:S(2)}) copy-start(bf16[2,4,256,128]{2,3,1,0:T(8,128)(2,1)} %copy-done.5) | copy-start | bytes 1572868
  104.8 12.0 %collective-permute-start.6 = (bf16[2,4,256]{2,1,0:T(4,128)(2,1)S(1)}, bf16[2,4,256]{2,1,0:T(4,128)(2,1)S(1)}, u32[]{:S(2)}, u32[]{:S(2)}) collective-permute-start(bf16[2,4,256]{2,1,0:T(4,128)(2,1)S(1)} %bitcast.156), channel_id=1, source_target_pairs={{0,1},{1,2},{2,3},{4,5},{5,6},{6,7},{8,9},{9,10},{10,11},{12,13},{... | collective-permute-start | bytes 12296 | tf_op jit(solution)/shard_map/ppermute | solution.py:141
  107.1 9.8 %collective-permute-start.7 = (bf16[2,4,256]{2,1,0:T(4,128)(2,1)S(1)}, bf16[2,4,256]{2,1,0:T(4,128)(2,1)S(1)}, u32[]{:S(2)}, u32[]{:S(2)}) collective-permute-start(bf16[2,4,256]{2,1,0:T(4,128)(2,1)S(1)} %bitcast.157), channel_id=1, source_target_pairs={{1,0},{2,1},{3,2},{5,4},{6,5},{7,6},{9,8},{10,9},{11,10},{13,12},{... | collective-permute-start | bytes 12296 | tf_op jit(solution)/shard_map/ppermute | solution.py:142
  109.2 25.6 %all-to-all-start.1 = ((bf16[2,4,16,16,128]{4,3,1,0,2:T(8,128)(2,1)}), bf16[2,4,16,16,128]{4,3,1,0,2:T(8,128)(2,1)S(1)}, u32[]{:S(2)}, u32[]{:S(2)}) async-start(bf16[2,4,16,16,128]{4,3,1,0,2:T(8,128)(2,1)} %copy.143), calls=%async_computation.1 | async-start | bytes 1048576 | tf_op jit(solution)/shard_map/all_to_all | solution.py:132
  117.2 1.0 copy-start.14
  117.2 1.1 copy-start.37
  134.8 21.5 %all-to-all-start.3 = ((bf16[2,4,16,16,128]{4,3,1,0,2:T(8,128)(2,1)}), bf16[2,4,16,16,128]{4,3,1,0,2:T(8,128)(2,1)}, u32[]{:S(2)}, u32[]{:S(2)}) async-start(bf16[2,4,16,16,128]{4,3,1,0,2:T(8,128)(2,1)} %copy.152), calls=%async_computation.3 | async-start | bytes 1048576 | tf_op jit(solution)/shard_map/all_to_all | solution.py:132
  139.3 3.1 %copy-start.1 = (bf16[2,16,16,512]{3,2,1,0:T(8,128)(2,1)S(1)}, bf16[2,16,16,512]{3,2,1,0:T(8,128)(2,1)}, u32[]{:S(2)}) copy-start(bf16[2,16,16,512]{3,2,1,0:T(8,128)(2,1)} %param.8) | copy-start | bytes 1572868
  139.3 3.1 %copy-start.11 = (f32[2,16,512]{2,1,0:T(8,128)S(1)}, f32[2,16,512]{2,1,0:T(8,128)}, u32[]{:S(2)}) copy-start(f32[2,16,512]{2,1,0:T(8,128)} %copy-done.10) | copy-start | bytes 196612
  139.3 3.1 %copy-start.12 = (f32[2,16,512]{2,1,0:T(8,128)S(1)}, f32[2,16,512]{2,1,0:T(8,128)}, u32[]{:S(2)}) copy-start(f32[2,16,512]{2,1,0:T(8,128)} %get-tuple-element.21) | copy-start | bytes 196612
  147.5 11.7 %collective-permute-start.2 = (f32[2,16,1,512]{3,2,1,0:T(1,128)S(1)}, f32[2,16,1,512]{3,2,1,0:T(1,128)S(1)}, u32[]{:S(2)}, u32[]{:S(2)}) collective-permute-start(f32[2,16,1,512]{3,2,1,0:T(1,128)S(1)} %get-tuple-element.27), channel_id=1, source_target_pairs={{16,0},{32,16},{48,32},{64,48},{80,64},{96,80},{112,96},{128,112},... | collective-permute-start | bytes 196616 | tf_op jit(solution)/shard_map/ppermute | solution.py:15
  149.4 9.8 %collective-permute-start.3 = (f32[2,16,1,512]{3,2,1,0:T(1,128)S(1)}, f32[2,16,1,512]{3,2,1,0:T(1,128)S(1)}, u32[]{:S(2)}, u32[]{:S(2)}) collective-permute-start(f32[2,16,1,512]{3,2,1,0:T(1,128)S(1)} %get-tuple-element.28), channel_id=1, source_target_pairs={{0,16},{16,32},{32,48},{48,64},{64,80},{80,96},{96,112},{112,128},... | collective-permute-start | bytes 196616 | tf_op jit(solution)/shard_map/ppermute | solution.py:14
  (2 other events, 1.8 us)

commit v2 on v1

--- a/solution.py
+++ b/solution.py
@@ -94,14 +94,9 @@
     leftward = [(b, a) for a, b in rightward]
 
     def pack(init_f):
-        top = init_f[:, 0 : rows : rows_c]
-        mid = init_f[:, 1 : rows + 1].reshape(fields, row_chunks, rows_c, modes_dev, cols)
-        bot = init_f[:, rows_c + 1 : rows + 2 : rows_c]
-        main = jnp.concatenate([top[:, :, None], mid, bot[:, :, None]], axis=2)
-        main = main.reshape(fields, row_chunks, rows_c + 2, modes_dev, col_chunks, LANES)
-        inner = init_f[:, 1 : rows + 1]
-        hl = jnp.pad(inner[..., LANES - 1 : cols - 1 : LANES], ((0, 0), (0, 0), (0, 0), (1, 0)))
-        hr = jnp.pad(inner[..., LANES : cols : LANES], ((0, 0), (0, 0), (0, 0), (0, 1)))
+        main = init_f.reshape(fields, row_chunks, rows_c, modes_dev, col_chunks, LANES)
+        hl = jnp.pad(init_f[..., LANES - 1 : cols - 1 : LANES], ((0, 0), (0, 0), (0, 0), (1, 0)))
+        hr = jnp.pad(init_f[..., LANES : cols : LANES], ((0, 0), (0, 0), (0, 0), (0, 1)))
         sides = []
         for h in (hl, hr):
             h = h.reshape(fields, row_chunks, rows_c, modes_dev, col_chunks)
@@ -115,9 +110,12 @@
         full = full.transpose(1, 4, 0, 2, 3, 5).reshape(devs, fields, -1, modes_dev, LANES)
         return lax.all_to_all(full, "modes", split_axis=0, concat_axis=3, tiled=True)[0]
 
-    got = pack(init_x)
-    padded = got[:, : rows_c + 2].astype(jnp.float32)
-    side = got[:, rows_c + 2].astype(jnp.float32)
+    got = pack(initial.transpose(0, 2, 1, 3))
+    inner0 = got[:, :rows_c]
+    low0 = lax.ppermute(inner0[:, -1:], flat, down)
+    high0 = lax.ppermute(inner0[:, :1], flat, up)
+    padded = jnp.concatenate([low0, inner0, high0], axis=1).astype(jnp.float32)
+    side = got[:, rows_c].astype(jnp.float32)
     fill_l = side[..., :rows_c].transpose(0, 2, 1)
     fill_r = side[..., rows_c : 2 * rows_c].transpose(0, 2, 1)
     code = side[0, :, 2 * rows_c : 2 * rows_c + 3 * width]
@@ -178,7 +176,7 @@
         lap_o = 4.0 * center - pad_o[:, :, 2:] - pad_o[:, :, :-2] - right - left
         resid = rhs_o - base_o * lap_o - coupled_owner[sweep].astype(jnp.float32)
         scaled = resid * inv_base_o
-        update = jnp.sum(own_inv[None, :, :, None, None] * scaled[:, None], axis=2)
+        update = jnp.einsum("ac,fcxy->faxy", own_inv, scaled, precision=lax.Precision.HIGHEST)
         u_o = u_o + 0.6 * update
     return u_o
 

time: 167 us -> 155 us (0.928)
  the two profiles are of different devices: /device:TPU:24 before, /device:TPU:27 now
where the time goes in v2:
time: 155 us; the launch traced here: 154 us
  starting transfers between devices  69.3 us (45%)
  local copies, waits for them, and re-layouts  36.4 us (23%)
  waiting for transfers between devices  29.8 us (19%)
  matrix products  11.3 us (7%)
  other arithmetic  6.83 us (4%)
    all_to_all x2, starting transfers between devices, to_owner(): lax.all_to_all(mixed, 'modes', split_axis=2, concat_axis=2, tiled=True)  17.4 us
    all_to_all x2, waiting for transfers between devices, to_owner(): lax.all_to_all(mixed, 'modes', split_axis=2, concat_axis=2, tiled=True)  17 us
    ppermute x2, starting transfers between devices, ring_halo(): lax.ppermute(lax.slice_in_dim(block, block.shape[dim] - 1, None, axis=dim...  11.9 us
    all_to_all x1, starting transfers between devices, sweeps(): lax.all_to_all(rp, 'modes', split_axis=0, concat_axis=3, tiled=True)[0]  11.7 us
    all_to_all x1, waiting for transfers between devices, pack(): lax.all_to_all(full, 'modes', split_axis=0, concat_axis=3, tiled=True)[0]  9.39 us
    dot_general x2, matrix products, sweeps(): jnp.einsum('ac,fcxy->faxy', own_inv, scaled, precision=lax.Precision.HIGH...  7.16 us
    unnamed x61, local copies, waits for them, and re-layouts  6.01 us
    all_to_all x1, starting transfers between devices, pack(): lax.all_to_all(full, 'modes', split_axis=0, concat_axis=3, tiled=True)[0]  5.48 us
  transfers between devices with their start and end apart: 14, of which 4 were waited for; matrix products, arithmetic and copies ran while one was open for 23% of the time, Pallas kernels for 0%

profile of v2, /device:TPU:27, one launch (start us, length us, event | category | flops | bytes accessed | tf_op | source)
XLA Modules:
  0.0 154.4 jit_solution(11780672523505914536)
XLA Ops:
  0.0 1.2 reshape.129
  1.2 1.2 copy.122
  2.4 11.7 %all-to-all-start.2 = ((bf16[16,2,4,16,128]{4,3,2,1,0:T(8,128)(2,1)}), bf16[16,2,4,16,128]{4,3,2,1,0:T(8,128)(2,1)S(1)}, u32[]{:S(2)}, u32[]{:S(2)}) async-start(bf16[16,2,4,16,128]{4,3,2,1,0:T(8,128)(2,1)} %bitcast.42), calls=%async_computation.2 | async-start | bytes 1048576 | tf_op jit(solution)/shard_map/all_to_all | solution.py:74
  14.5 6.1 %collective-permute-start = (bf16[2,1,16,512]{3,2,1,0:T(8,128)(2,1)S(1)}, bf16[2,1,16,512]{3,2,1,0:T(8,128)(2,1)S(1)}, u32[]{:S(2)}, u32[]{:S(2)}) collective-permute-start(bf16[2,1,16,512]{3,2,1,0:T(8,128)(2,1)S(1)} %get-tuple-element.40), channel_id=1, source_target_pairs={{0,16},{16,32},{32,48},{48,64},{64,80},{80,96},{96,112},{112,128},... | collective-permute-start | bytes 98312 | tf_op jit(solution)/shard_map/ppermute | solution.py:14
  20.6 1.9 %collective-permute-start.1 = (bf16[2,1,16,512]{3,2,1,0:T(8,128)(2,1)S(1)}, bf16[2,1,16,512]{3,2,1,0:T(8,128)(2,1)S(1)}, u32[]{:S(2)}, u32[]{:S(2)}) collective-permute-start(bf16[2,1,16,512]{3,2,1,0:T(8,128)(2,1)S(1)} %get-tuple-element.41), channel_id=1, source_target_pairs={{16,0},{32,16},{48,32},{64,48},{80,64},{96,80},{112,96},{128,112},... | collective-permute-start | bytes 98312 | tf_op jit(solution)/shard_map/ppermute | solution.py:15
  23.9 0.9 copy.110
  24.8 0.9 copy.111
  26.6 0.9 copy.112
  28.0 3.3 %all-to-all-done.2 = bf16[16,2,4,16,128]{4,3,2,1,0:T(8,128)(2,1)S(1)} async-done(((bf16[16,2,4,16,128]{4,3,2,1,0:T(8,128)(2,1)}), bf16[16,2,4,16,128]{4,3,2,1,0:T(8,128)(2,1)S(1)}, u32[]{:S(2)}, u32[]{:S(2)}) %all-to-all-start.2) | async-done | bytes 524320 | tf_op jit(solution)/shard_map/all_to_all | solution.py:74
  31.3 5.5 %all-to-all-start = ((bf16[16,2,5,16,128]{4,3,2,1,0:T(8,128)(2,1)}), bf16[16,2,5,16,128]{4,3,2,1,0:T(8,128)(2,1)}, u32[]{:S(2)}, u32[]{:S(2)}) async-start(bf16[16,2,5,16,128]{4,3,2,1,0:T(8,128)(2,1)} %bitcast.18), calls=%async_computation | async-start | bytes 1310720 | tf_op jit(solution)/shard_map/all_to_all | solution.py:111
  38.9 0.7 multiply_divide_fusion
  40.8 3.7 %mul.583 = bf16[3,256,256]{2,1,0:T(8,128)(2,1)} reshape(bf16[3,16,16,16,16]{4,3,2,1,0:T(8,128)(2,1)S(1)} %mul.582) | data formatting | bytes 786432 | tf_op jit(solution)/shard_map/mul | solution.py:39
  44.5 1.2 convert_bitcast_fusion
  45.8 1.3 copy.124
  47.1 9.4 %all-to-all-done = bf16[16,2,5,16,128]{4,3,2,1,0:T(8,128)(2,1)} async-done(((bf16[16,2,5,16,128]{4,3,2,1,0:T(8,128)(2,1)}), bf16[16,2,5,16,128]{4,3,2,1,0:T(8,128)(2,1)}, u32[]{:S(2)}, u32[]{:S(2)}) %all-to-all-start) | async-done | bytes 655392 | tf_op jit(solution)/shard_map/all_to_all | solution.py:111
  56.5 1.2 copy.113
  57.8 0.8 copy.141
  58.6 3.6 %collective-permute-start.2 = (bf16[2,1,256,128]{2,3,1,0:T(8,128)(2,1)}, bf16[2,1,256,128]{2,3,1,0:T(8,128)(2,1)}, u32[]{:S(2)}, u32[]{:S(2)}) collective-permute-start(bf16[2,1,256,128]{2,3,1,0:T(8,128)(2,1)} %copy.141), channel_id=1, source_target_pairs={{0,4},{1,5},{2,6},{3,7},{4,8},{5,9},{6,10},{7,11},{8,12},{9,13},{1... | collective-permute-start | bytes 393224 | tf_op jit(solution)/shard_map/ppermute | solution.py:115
  62.1 0.8 copy.143
  62.9 4.1 %collective-permute-start.3 = (bf16[2,1,256,128]{2,3,1,0:T(8,128)(2,1)}, bf16[2,1,256,128]{2,3,1,0:T(8,128)(2,1)}, u32[]{:S(2)}, u32[]{:S(2)}) collective-permute-start(bf16[2,1,256,128]{2,3,1,0:T(8,128)(2,1)} %copy.143), channel_id=1, source_target_pairs={{4,0},{5,1},{6,2},{7,3},{8,4},{9,5},{10,6},{11,7},{12,8},{13,9},{1... | collective-permute-start | bytes 393224 | tf_op jit(solution)/shard_map/ppermute | solution.py:116
  67.0 1.0 copy.142
  69.2 0.8 slice_bitcast_fusion.1
  70.6 0.9 reshape.144
  71.5 1.3 maximum_convert_fusion
  73.8 1.0 copy-done.2
  75.4 1.0 copy.119
  76.4 2.9 %fusion.13 = bf16[2,4,256,128]{2,3,1,0:T(8,128)(2,1)S(1)} fusion(bf16[2,4,256,128]{2,3,1,0:T(8,128)(2,1)} %copy-done.6, f32[2,4,256,128]{2,3,1,0:T(8,128)} %copy.124, f32[2,4,256,128]{2,3,1,0:T(8,128)} %copy-done.2, f32[2,6,256,128]{2,3,1,0:T(8,128)S(1)} %maximum_convert_fusion, f32[2,4,128]{2,1,0:T(4,128)S(1)} %copy-done.23, ...), kind=kOutput, calls=%fused_computation.18 | convolution fusion | flops 807403520 | bytes 4464640 | tf_op jit(solution)/shard_map/ij,fxjy->fxiy/dot_general | solution.py:158
  79.3 4.8 %collective-permute-start.6 = (bf16[2,1,256,128]{2,3,1,0:T(8,128)(2,1)S(1)}, bf16[2,1,256,128]{2,3,1,0:T(8,128)(2,1)S(1)}, u32[]{:S(2)}, u32[]{:S(2)}) collective-permute-start(bf16[2,1,256,128]{2,3,1,0:T(8,128)(2,1)S(1)} %get-tuple-element.38), channel_id=1, source_target_pairs={{0,4},{1,5},{2,6},{3,7},{4,8},{5,9},{6,10},{7,11},{8,12},{9,13},{1... | collective-permute-start | bytes 393224 | tf_op jit(solution)/shard_map/ppermute | solution.py:137
  84.2 2.8 %collective-permute-start.7 = (bf16[2,1,256,128]{2,3,1,0:T(8,128)(2,1)S(1)}, bf16[2,1,256,128]{2,3,1,0:T(8,128)(2,1)S(1)}, u32[]{:S(2)}, u32[]{:S(2)}) collective-permute-start(bf16[2,1,256,128]{2,3,1,0:T(8,128)(2,1)S(1)} %get-tuple-element.39), channel_id=1, source_target_pairs={{4,0},{5,1},{6,2},{7,3},{8,4},{9,5},{10,6},{11,7},{12,8},{13,9},{1... | collective-permute-start | bytes 393224 | tf_op jit(solution)/shard_map/ppermute | solution.py:138
  87.1 2.4 %collective-permute-start.8 = (bf16[2,4,256]{2,1,0:T(4,128)(2,1)S(1)}, bf16[2,4,256]{2,1,0:T(4,128)(2,1)S(1)}, u32[]{:S(2)}, u32[]{:S(2)}) collective-permute-start(bf16[2,4,256]{2,1,0:T(4,128)(2,1)S(1)} %bitcast.168), channel_id=1, source_target_pairs={{0,1},{1,2},{2,3},{4,5},{5,6},{6,7},{8,9},{9,10},{10,11},{12,13},{... | collective-permute-start | bytes 12296 | tf_op jit(solution)/shard_map/ppermute | solution.py:139
  89.5 1.3 collective-permute-start.9
  90.8 0.9 copy.120
  91.6 13.8 %all-to-all-start.1 = ((bf16[2,4,16,16,128]{4,3,1,0,2:T(8,128)(2,1)}), bf16[2,4,16,16,128]{4,3,1,0,2:T(8,128)(2,1)S(1)}, u32[]{:S(2)}, u32[]{:S(2)}) async-start(bf16[2,4,16,16,128]{4,3,1,0,2:T(8,128)(2,1)} %copy.120), calls=%async_computation.1 | async-start | bytes 1048576 | tf_op jit(solution)/shard_map/all_to_all | solution.py:130
  106.3 0.7 copy-done.14
  108.1 0.9 copy.129
  109.0 15.4 %all-to-all-done.1 = bf16[2,4,16,16,128]{4,3,1,0,2:T(8,128)(2,1)S(1)} async-done(((bf16[2,4,16,16,128]{4,3,1,0,2:T(8,128)(2,1)}), bf16[2,4,16,16,128]{4,3,1,0,2:T(8,128)(2,1)S(1)}, u32[]{:S(2)}, u32[]{:S(2)}) %all-to-all-start.1) | async-done | bytes 524320 | tf_op jit(solution)/shard_map/all_to_all | solution.py:130
  124.3 3.6 %all-to-all-start.3 = ((bf16[2,4,16,16,128]{4,3,1,0,2:T(8,128)(2,1)}), bf16[2,4,16,16,128]{4,3,1,0,2:T(8,128)(2,1)S(1)}, u32[]{:S(2)}, u32[]{:S(2)}) async-start(bf16[2,4,16,16,128]{4,3,1,0,2:T(8,128)(2,1)} %copy.129), calls=%async_computation.3 | async-start | bytes 1048576 | tf_op jit(solution)/shard_map/all_to_all | solution.py:130
  127.9 1.7 %fusion.90 = (f32[2,16,16,511]{3,1,2,0:T(8,128)}, f32[2,16,16,511]{3,1,2,0:T(8,128)}) fusion(f32[2,16,18,512]{3,1,2,0:T(8,128)S(1)} %convert_bitcast_fusion), kind=kLoop, calls=%fused_computation.149 | loop fusion | bytes 4186112 | tf_op jit(solution)/shard_map/slice | solution.py:174
  129.6 1.5 copy.158
  131.2 1.4 reshape.133
  132.6 3.6 %fusion.9 = f32[2,16,16,512]{3,1,2,0:T(8,128)S(1)} fusion(f32[2,16,16,512]{3,1,2,0:T(8,128)} %reshape.133, f32[2,16,18,512]{3,1,2,0:T(8,128)S(1)} %convert_bitcast_fusion, f32[2,16,16,511]{3,1,2,0:T(8,128)} %get-tuple-element.26, f32[2,16,16,511]{3,1,2,0:T(8,128)} %get-tuple-element.25, f32[2,16,512]{2,1,0:T(8,128)S(1)} %copy-done.10, ...), kind=kOutput, calls=%fused_computation.13 | convolution fusion | flops 53477376 | bytes 9048064 | tf_op jit(solution)/shard_map/ac,fcxy->faxy/dot_general | solution.py:179
  136.2 1.9 %collective-permute-start.4 = (f32[2,16,1,512]{3,1,2,0:T(8,128)S(1)}, f32[2,16,1,512]{3,1,2,0:T(8,128)S(1)}, u32[]{:S(2)}, u32[]{:S(2)}) collective-permute-start(f32[2,16,1,512]{3,1,2,0:T(8,128)S(1)} %get-tuple-element.29), channel_id=1, source_target_pairs={{16,0},{32,16},{48,32},{64,48},{80,64},{96,80},{112,96},{128,112},... | collective-permute-start | bytes 196616 | tf_op jit(solution)/shard_map/ppermute | solution.py:15
  138.1 5.8 %collective-permute-start.5 = (f32[2,16,1,512]{3,1,2,0:T(8,128)S(1)}, f32[2,16,1,512]{3,1,2,0:T(8,128)S(1)}, u32[]{:S(2)}, u32[]{:S(2)}) collective-permute-start(f32[2,16,1,512]{3,1,2,0:T(8,128)S(1)} %get-tuple-element.30), channel_id=1, source_target_pairs={{0,16},{16,32},{32,48},{48,64},{64,80},{80,96},{96,112},{112,128},... | collective-permute-start | bytes 196616 | tf_op jit(solution)/shard_map/ppermute | solution.py:14
  143.8 1.7 %fusion.91 = (f32[2,16,16,511]{3,1,2,0:T(8,128)}, f32[2,16,16,511]{3,1,2,0:T(8,128)}) fusion(f32[2,16,16,512]{3,1,2,0:T(8,128)S(1)} %fusion.9), kind=kLoop, calls=%fused_computation.150 | loop fusion | bytes 4186112 | tf_op jit(solution)/shard_map/slice | solution.py:174
  145.5 1.7 %all-to-all-done.3 = bf16[2,4,16,16,128]{4,3,1,0,2:T(8,128)(2,1)S(1)} async-done(((bf16[2,4,16,16,128]{4,3,1,0,2:T(8,128)(2,1)}), bf16[2,4,16,16,128]{4,3,1,0,2:T(8,128)(2,1)S(1)}, u32[]{:S(2)}, u32[]{:S(2)}) %all-to-all-start.3) | async-done | bytes 524320 | tf_op jit(solution)/shard_map/all_to_all | solution.py:130
  147.8 1.4 reshape.137
  149.2 3.6 %fusion.7 = f32[2,16,16,512]{3,1,2,0:T(8,128)S(1)} fusion(f32[2,16,16,512]{3,1,2,0:T(8,128)S(1)} %fusion.9, f32[2,16,16,512]{3,1,2,0:T(8,128)} %reshape.137, f32[2,16,1,512]{3,1,2,0:T(8,128)S(1)} %collective-permute-done.5, f32[2,16,1,512]{3,1,2,0:T(8,128)S(1)} %collective-permute-done.4, f32[2,16,16,511]{3,1,2,0:T(8,128)} %get-tuple-element.28, ...), kind=kOutput, calls=%fused_computation.10 | convolution fusion | flops 54001664 | bytes 6026240 | tf_op jit(solution)/shard_map/ac,fcxy->faxy/dot_general | solution.py:179
  152.8 1.6 %copy.132 = f32[2,16,16,512]{3,2,1,0:T(8,128)} copy(f32[2,16,16,512]{3,1,2,0:T(8,128)S(1)} %fusion.7) | data formatting | bytes 2097152 | tf_op jit(solution)/shard_map/add | solution.py:180
  (130 shorter events, 12.1 us)
Async XLA Ops:
  0.0 14.1 %copy-start.11 = (bf16[2,16,16,512]{3,2,1,0:T(8,128)(2,1)S(1)}, bf16[2,16,16,512]{3,2,1,0:T(8,128)(2,1)}, u32[]{:S(2)}) copy-start(bf16[2,16,16,512]{3,2,1,0:T(8,128)(2,1)} %param.9) | copy-start | bytes 1572868
  1.2 21.3 %copy-start.15 = (f32[1,16,16]{2,1,0:T(8,128)S(1)}, f32[1,16,16]{2,1,0:T(8,128)}, u32[]{:S(2)}) copy-start(f32[1,16,16]{2,1,0:T(8,128)} %param.15) | copy-start | bytes 3076
  2.4 28.9 %all-to-all-start.2 = ((bf16[16,2,4,16,128]{4,3,2,1,0:T(8,128)(2,1)}), bf16[16,2,4,16,128]{4,3,2,1,0:T(8,128)(2,1)S(1)}, u32[]{:S(2)}, u32[]{:S(2)}) async-start(bf16[16,2,4,16,128]{4,3,2,1,0:T(8,128)(2,1)} %bitcast.42), calls=%async_computation.2 | async-start | bytes 1048576 | tf_op jit(solution)/shard_map/all_to_all | solution.py:74
  14.4 11.8 %copy-start = (bf16[2,16,16,512]{3,1,2,0:T(8,128)(2,1)}, bf16[2,16,16,512]{3,1,2,0:T(8,128)(2,1)S(1)}, u32[]{:S(2)}) copy-start(bf16[2,16,16,512]{3,1,2,0:T(8,128)(2,1)S(1)} %copy.159) | copy-start | bytes 1572868
  14.5 30.0 %collective-permute-start = (bf16[2,1,16,512]{3,2,1,0:T(8,128)(2,1)S(1)}, bf16[2,1,16,512]{3,2,1,0:T(8,128)(2,1)S(1)}, u32[]{:S(2)}, u32[]{:S(2)}) collective-permute-start(bf16[2,1,16,512]{3,2,1,0:T(8,128)(2,1)S(1)} %get-tuple-element.40), channel_id=1, source_target_pairs={{0,16},{16,32},{32,48},{48,64},{64,80},{80,96},{96,112},{112,128},... | collective-permute-start | bytes 98312 | tf_op jit(solution)/shard_map/ppermute | solution.py:14
  20.6 23.9 %collective-permute-start.1 = (bf16[2,1,16,512]{3,2,1,0:T(8,128)(2,1)S(1)}, bf16[2,1,16,512]{3,2,1,0:T(8,128)(2,1)S(1)}, u32[]{:S(2)}, u32[]{:S(2)}) collective-permute-start(bf16[2,1,16,512]{3,2,1,0:T(8,128)(2,1)S(1)} %get-tuple-element.41), channel_id=1, source_target_pairs={{16,0},{32,16},{48,32},{64,48},{80,64},{96,80},{112,96},{128,112},... | collective-permute-start | bytes 98312 | tf_op jit(solution)/shard_map/ppermute | solution.py:15
  25.8 1.8 %copy-start.17 = (f32[2,8]{1,0:T(2,128)S(1)}, f32[2,8]{1,0:T(2,128)}, u32[]{:S(2)}) copy-start(f32[2,8]{1,0:T(2,128)} %param.11) | copy-start | bytes 196
  25.8 2.1 %copy-start.16 = (f32[2,3,8]{2,0,1:T(2,128)S(1)}, f32[2,3,8]{2,0,1:T(2,128)}, u32[]{:S(2)}) copy-start(f32[2,3,8]{2,0,1:T(2,128)} %param.12) | copy-start | bytes 580
  25.8 2.1 %copy-start.19 = (s32[16,512]{1,0:T(8,128)S(1)}, s32[16,512]{1,0:T(8,128)}, u32[]{:S(2)}) copy-start(s32[16,512]{1,0:T(8,128)} %param.10) | copy-start | bytes 98308
  27.6 12.7 %copy-start.20 = (s32[3,16,16]{2,1,0:T(8,128)S(1)}, s32[3,16,16]{2,1,0:T(8,128)}, u32[]{:S(2)}) copy-start(s32[3,16,16]{2,1,0:T(8,128)} %param.14) | copy-start | bytes 9220
  31.3 9.0 %copy-start.3 = (bf16[16,2,4,16,128]{4,3,2,1,0:T(8,128)(2,1)}, bf16[16,2,4,16,128]{4,3,2,1,0:T(8,128)(2,1)S(1)}, u32[]{:S(2)}) copy-start(bf16[16,2,4,16,128]{4,3,2,1,0:T(8,128)(2,1)S(1)} %all-to-all-done.2) | copy-start | bytes 1572868
  31.3 25.2 %all-to-all-start = ((bf16[16,2,5,16,128]{4,3,2,1,0:T(8,128)(2,1)}), bf16[16,2,5,16,128]{4,3,2,1,0:T(8,128)(2,1)}, u32[]{:S(2)}, u32[]{:S(2)}) async-start(bf16[16,2,5,16,128]{4,3,2,1,0:T(8,128)(2,1)} %bitcast.18), calls=%async_computation | async-start | bytes 1310720 | tf_op jit(solution)/shard_map/all_to_all | solution.py:111
  39.6 0.7 copy-start.8
  44.5 1.2 copy-start.4
  58.6 12.9 %collective-permute-start.2 = (bf16[2,1,256,128]{2,3,1,0:T(8,128)(2,1)}, bf16[2,1,256,128]{2,3,1,0:T(8,128)(2,1)}, u32[]{:S(2)}, u32[]{:S(2)}) collective-permute-start(bf16[2,1,256,128]{2,3,1,0:T(8,128)(2,1)} %copy.141), channel_id=1, source_target_pairs={{0,4},{1,5},{2,6},{3,7},{4,8},{5,9},{6,10},{7,11},{8,12},{9,13},{1... | collective-permute-start | bytes 393224 | tf_op jit(solution)/shard_map/ppermute | solution.py:115
  62.9 8.6 %collective-permute-start.3 = (bf16[2,1,256,128]{2,3,1,0:T(8,128)(2,1)}, bf16[2,1,256,128]{2,3,1,0:T(8,128)(2,1)}, u32[]{:S(2)}, u32[]{:S(2)}) collective-permute-start(bf16[2,1,256,128]{2,3,1,0:T(8,128)(2,1)} %copy.143), channel_id=1, source_target_pairs={{4,0},{5,1},{6,2},{7,3},{8,4},{9,5},{10,6},{11,7},{12,8},{13,9},{1... | collective-permute-start | bytes 393224 | tf_op jit(solution)/shard_map/ppermute | solution.py:116
  68.2 0.7 copy-start.12
  72.8 0.7 copy-start.18
  73.5 1.3 copy-start.13
  73.5 1.3 copy-start.21
  73.5 1.3 copy-start.25
  73.8 1.0 copy-start.2
  74.8 1.7 %copy-start.23 = (f32[2,4,128]{2,1,0:T(4,128)S(1)}, f32[2,4,128]{2,1,0:T(4,128)}, u32[]{:S(2)}) copy-start(f32[2,4,128]{2,1,0:T(4,128)} %get-tuple-element.19) | copy-start | bytes 12292
  74.8 1.7 %copy-start.24 = (f32[2,4,128]{2,1,0:T(4,128)S(1)}, f32[2,4,128]{2,1,0:T(4,128)}, u32[]{:S(2)}) copy-start(f32[2,4,128]{2,1,0:T(4,128)} %get-tuple-element.20) | copy-start | bytes 12292
  75.4 1.0 copy-start.6
  76.4 14.3 %copy-start.7 = (bf16[2,4,256,128]{3,2,1,0:T(8,128)(2,1)S(1)}, bf16[2,4,256,128]{3,2,1,0:T(8,128)(2,1)}, u32[]{:S(2)}) copy-start(bf16[2,4,256,128]{3,2,1,0:T(8,128)(2,1)} %copy.119) | copy-start | bytes 1572868
  79.3 26.1 %collective-permute-start.6 = (bf16[2,1,256,128]{2,3,1,0:T(8,128)(2,1)S(1)}, bf16[2,1,256,128]{2,3,1,0:T(8,128)(2,1)S(1)}, u32[]{:S(2)}, u32[]{:S(2)}) collective-permute-start(bf16[2,1,256,128]{2,3,1,0:T(8,128)(2,1)S(1)} %get-tuple-element.38), channel_id=1, source_target_pairs={{0,4},{1,5},{2,6},{3,7},{4,8},{5,9},{6,10},{7,11},{8,12},{9,13},{1... | collective-permute-start | bytes 393224 | tf_op jit(solution)/shard_map/ppermute | solution.py:137
  84.2 21.3 %collective-permute-start.7 = (bf16[2,1,256,128]{2,3,1,0:T(8,128)(2,1)S(1)}, bf16[2,1,256,128]{2,3,1,0:T(8,128)(2,1)S(1)}, u32[]{:S(2)}, u32[]{:S(2)}) collective-permute-start(bf16[2,1,256,128]{2,3,1,0:T(8,128)(2,1)S(1)} %get-tuple-element.39), channel_id=1, source_target_pairs={{4,0},{5,1},{6,2},{7,3},{8,4},{9,5},{10,6},{11,7},{12,8},{13,9},{1... | collective-permute-start | bytes 393224 | tf_op jit(solution)/shard_map/ppermute | solution.py:138
  87.1 18.5 %collective-permute-start.8 = (bf16[2,4,256]{2,1,0:T(4,128)(2,1)S(1)}, bf16[2,4,256]{2,1,0:T(4,128)(2,1)S(1)}, u32[]{:S(2)}, u32[]{:S(2)}) collective-permute-start(bf16[2,4,256]{2,1,0:T(4,128)(2,1)S(1)} %bitcast.168), channel_id=1, source_target_pairs={{0,1},{1,2},{2,3},{4,5},{5,6},{6,7},{8,9},{9,10},{10,11},{12,13},{... | collective-permute-start | bytes 12296 | tf_op jit(solution)/shard_map/ppermute | solution.py:139
  89.5 16.2 %collective-permute-start.9 = (bf16[2,4,256]{2,1,0:T(4,128)(2,1)S(1)}, bf16[2,4,256]{2,1,0:T(4,128)(2,1)S(1)}, u32[]{:S(2)}, u32[]{:S(2)}) collective-permute-start(bf16[2,4,256]{2,1,0:T(4,128)(2,1)S(1)} %bitcast.169), channel_id=1, source_target_pairs={{1,0},{2,1},{3,2},{5,4},{6,5},{7,6},{9,8},{10,9},{11,10},{13,12},{... | collective-permute-start | bytes 12296 | tf_op jit(solution)/shard_map/ppermute | solution.py:140
  91.6 32.7 %all-to-all-start.1 = ((bf16[2,4,16,16,128]{4,3,1,0,2:T(8,128)(2,1)}), bf16[2,4,16,16,128]{4,3,1,0,2:T(8,128)(2,1)S(1)}, u32[]{:S(2)}, u32[]{:S(2)}) async-start(bf16[2,4,16,16,128]{4,3,1,0,2:T(8,128)(2,1)} %copy.120), calls=%async_computation.1 | async-start | bytes 1048576 | tf_op jit(solution)/shard_map/all_to_all | solution.py:130
  106.0 1.0 copy-start.14
  106.0 1.0 copy-start.22
  106.0 1.1 copy-start.26
  124.3 5.3 %copy-start.5 = (bf16[2,4,16,16,128]{4,3,1,0,2:T(8,128)(2,1)}, bf16[2,4,16,16,128]{4,3,1,0,2:T(8,128)(2,1)S(1)}, u32[]{:S(2)}) copy-start(bf16[2,4,16,16,128]{4,3,1,0,2:T(8,128)(2,1)S(1)} %all-to-all-done.1) | copy-start | bytes 1572868
  124.3 22.9 %all-to-all-start.3 = ((bf16[2,4,16,16,128]{4,3,1,0,2:T(8,128)(2,1)}), bf16[2,4,16,16,128]{4,3,1,0,2:T(8,128)(2,1)S(1)}, u32[]{:S(2)}, u32[]{:S(2)}) async-start(bf16[2,4,16,16,128]{4,3,1,0,2:T(8,128)(2,1)} %copy.129), calls=%async_computation.3 | async-start | bytes 1048576 | tf_op jit(solution)/shard_map/all_to_all | solution.py:130
  129.6 2.9 %copy-start.1 = (bf16[2,16,16,512]{3,2,1,0:T(8,128)(2,1)S(1)}, bf16[2,16,16,512]{3,2,1,0:T(8,128)(2,1)}, u32[]{:S(2)}) copy-start(bf16[2,16,16,512]{3,2,1,0:T(8,128)(2,1)} %param.8) | copy-start | bytes 1572868
  129.6 2.9 %copy-start.9 = (f32[2,16,512]{2,1,0:T(8,128)S(1)}, f32[2,16,512]{2,1,0:T(8,128)}, u32[]{:S(2)}) copy-start(f32[2,16,512]{2,1,0:T(8,128)} %copy-done.8) | copy-start | bytes 196612
  129.6 2.9 %copy-start.10 = (f32[2,16,512]{2,1,0:T(8,128)S(1)}, f32[2,16,512]{2,1,0:T(8,128)}, u32[]{:S(2)}) copy-start(f32[2,16,512]{2,1,0:T(8,128)} %get-tuple-element.21) | copy-start | bytes 196612
  136.2 13.0 %collective-permute-start.4 = (f32[2,16,1,512]{3,1,2,0:T(8,128)S(1)}, f32[2,16,1,512]{3,1,2,0:T(8,128)S(1)}, u32[]{:S(2)}, u32[]{:S(2)}) collective-permute-start(f32[2,16,1,512]{3,1,2,0:T(8,128)S(1)} %get-tuple-element.29), channel_id=1, source_target_pairs={{16,0},{32,16},{48,32},{64,48},{80,64},{96,80},{112,96},{128,112},... | collective-permute-start | bytes 196616 | tf_op jit(solution)/shard_map/ppermute | solution.py:15
  138.1 11.1 %collective-permute-start.5 = (f32[2,16,1,512]{3,1,2,0:T(8,128)S(1)}, f32[2,16,1,512]{3,1,2,0:T(8,128)S(1)}, u32[]{:S(2)}, u32[]{:S(2)}) collective-permute-start(f32[2,16,1,512]{3,1,2,0:T(8,128)S(1)} %get-tuple-element.30), channel_id=1, source_target_pairs={{0,16},{16,32},{32,48},{48,64},{64,80},{80,96},{96,112},{112,128},... | collective-permute-start | bytes 196616 | tf_op jit(solution)/shard_map/ppermute | solution.py:14
